TPU v7x, 256 devices: a whole 4x4x8 slice. The times are simulated.
256 devices in a mesh: pair: 32 (over x, z), vir: 8 (over y, core).
Axes of the slice: x: 4, y: 4, z: 8, core: 2. Of those that a mesh axis runs over, the one named last changes fastest.
Arguments:
- amplitudes: float32 [24576, 4096], P(('pair', 'vir')), may hold values from -6 to 6
- integrals: float32 [1536, 1536], P('vir'), may hold values from -0.15625 to 0.15625
- tile_owner: int32 [24576], P(('pair', 'vir')), may hold values from 0 to 31, as said below
- tile_key: int32 [24576], P(('pair', 'vir')), may hold values from 0 to 575
Outputs:
- residual: float32 [24576, 4096], P(('pair', 'vir'))
Inputs may be any that keep to these rules, and one draw needn't show every extreme that they name: `tile_owner`: among the 96 tiles of one device no owner is named more than 6 times; one owner, the same for every device, is named exactly 6 times by each device.
All inputs are finite; a program needn't handle non-finite values.
Results may differ from a plain program's by a relative error of at most 0.0003.
Values sent between devices are 32-bit elements; how exact they have to be, the bound alone decides.
No kernel may reach another device: no remote copies, remote signals or barrier semaphores. Data moves between devices by JAX's collectives and lax.ppermute only.
A program may use at most 128 MiB of HBM per device.

v0:
```python
import jax
import jax.numpy as jnp
from jax import lax
from jax.sharding import PartitionSpec as P

TS = 64
NS = 24
ROWSETS_DEV = 24


def per_device(amplitudes, integrals, tile_owner, tile_key):
    owner_count = lax.axis_size("pair")
    capacity = max(2, 2 * amplitudes.shape[0] // owner_count)
    picked = (tile_owner[:, None] == jnp.arange(owner_count, dtype=jnp.int32)[None, :]).astype(
        jnp.int32
    )
    before = jnp.cumsum(picked, axis=0) - picked
    slot_index = jnp.sum(before * picked, axis=1)
    send_tiles = (
        jnp.zeros((owner_count, capacity, TS * TS), jnp.float32)
        .at[tile_owner, slot_index]
        .set(amplitudes)
    )
    send_keys = (
        jnp.zeros((owner_count, capacity), jnp.int32).at[tile_owner, slot_index].set(tile_key)
    )
    recv_tiles, recv_keys = (
        lax.all_to_all(send_tiles, "pair", split_axis=0, concat_axis=0, tiled=True),
        lax.all_to_all(send_keys, "pair", split_axis=0, concat_axis=0, tiled=True),
    )
    arrived = recv_tiles.reshape(owner_count * capacity, TS, TS)
    flat_keys = recv_keys.reshape(owner_count * capacity)
    row_block = flat_keys // NS
    col_block = flat_keys % NS
    blocked = (
        jnp.zeros((ROWSETS_DEV, TS, NS, TS), jnp.float32)
        .at[row_block, :, col_block, :]
        .add(arrived)
    )
    blocked = blocked.reshape(ROWSETS_DEV * TS, NS * TS)
    product = jnp.dot(
        blocked,
        lax.all_gather(integrals, "vir", axis=0, tiled=True),
        precision=lax.Precision.HIGHEST,
        preferred_element_type=jnp.float32,
    )
    product = product.reshape(ROWSETS_DEV, TS, NS, TS)
    answers = product[row_block, :, col_block, :].reshape(owner_count, capacity, TS * TS)
    returned = lax.all_to_all(answers, "pair", split_axis=0, concat_axis=0, tiled=True)
    return returned[tile_owner, slot_index]


def solution(mesh):
    placed = (P(("pair", "vir"), None), P("vir", None), P(("pair", "vir")), P(("pair", "vir")))
    return jax.shard_map(
        per_device, mesh=mesh, in_specs=placed, out_specs=P(("pair", "vir"), None), check_vma=False
    )
```

profile of v0, /device:TPU:16, one launch (start us, length us, event | category | flops | bytes accessed | tf_op | source)
XLA Modules:
  0.0 476.3 jit_solution(556836381541302234)
XLA Ops:
  6.5 0.7 all-gather.2.cloned.1.call-update
  7.3 0.7 fusion.2
  8.1 0.8 select_reduce_fusion
  9.0 0.7 fusion.7
  9.7 8.3 %scatter_fusion = s32[32,6]{0,1:T(8,128)S(1)} fusion(s32[32,6]{0,1:T(8,128)S(1)} %broadcast_in_dim.9, s32[96]{0:T(128)S(1)} %get-tuple-element.11, s32[96]{0:T(128)} %param.7), kind=kCustom, calls=%fused_computation.2 | custom fusion | bytes 1920 | tf_op jit(solution)/shard_map/scatter | solution.py:25
  18.0 0.7 copy.14
  18.7 11.3 %all-to-all-start = ((s32[32,1,6]{2,1,0:T(1,128)}), s32[32,1,6]{2,1,0:T(1,128)S(1)}, u32[]{:S(2)}, u32[]{:S(2)}) async-start(s32[32,1,6]{2,1,0:T(1,128)} %copy.14), calls=%async_computation | async-start | bytes 32768 | tf_op jit(solution)/shard_map/all_to_all | solution.py:29
  30.0 0.3 broadcast_in_dim.11
  30.4 15.4 %scatter_fusion.1 = f32[32,6,4096]{2,0,1:T(8,128)S(1)} fusion(f32[32,6,4096]{2,0,1:T(8,128)S(1)} %broadcast_in_dim.11, s32[96]{0:T(128)S(1)} %get-tuple-element.11, f32[96,4096]{1,0:T(8,128)} %param.4), kind=kCustom, calls=%fused_computation.3 | custom fusion | bytes 4719360 | tf_op jit(solution)/shard_map/scatter | solution.py:22
  45.8 3.8 copy.15
  49.6 10.1 %all-to-all-start.1 = ((f32[32,6,4096]{2,1,0:T(8,128)}), f32[32,6,4096]{2,1,0:T(8,128)}, u32[]{:S(2)}, u32[]{:S(2)}) async-start(f32[32,6,4096]{2,1,0:T(8,128)} %copy.15), calls=%async_computation.1 | async-start | bytes 8388608 | tf_op jit(solution)/shard_map/all_to_all | solution.py:28
  60.3 95.7 %all-to-all-done.1 = f32[32,6,4096]{2,1,0:T(8,128)} async-done(((f32[32,6,4096]{2,1,0:T(8,128)}), f32[32,6,4096]{2,1,0:T(8,128)}, u32[]{:S(2)}, u32[]{:S(2)}) %all-to-all-start.1) | async-done | bytes 3145760 | tf_op jit(solution)/shard_map/all_to_all | solution.py:28
  156.0 6.8 %reshape.142 = f32[192,64,64]{2,1,0:T(8,128)} reshape(f32[32,6,4096]{2,1,0:T(8,128)} %all-to-all-done.1) | data formatting | bytes 6291456 | tf_op jit(solution)/shard_map/reshape | solution.py:31
  162.8 9.0 %broadcast_in_dim.8 = f32[24,64,24,64]{3,1,2,0:T(8,128)} broadcast(f32[]{:T(128)} %constant.16.clone.1), dimensions={} | broadcast | bytes 9437188 | tf_op jit(solution)/shard_map/broadcast_in_dim | solution.py:36
  171.8 31.4 %scatter_fusion.2 = f32[24,64,24,64]{3,1,2,0:T(8,128)} fusion(f32[24,64,24,64]{3,1,2,0:T(8,128)} %broadcast_in_dim.8, s32[192]{0:T(256)S(1)} %bitcast.38, f32[192,64,64]{2,1,0:T(8,128)} %reshape.142), kind=kCustom, calls=%fused_computation.4 | custom fusion | flops 786432 | bytes 9438720 | tf_op jit(solution)/shard_map/scatter-add | solution.py:38
  203.2 19.8 %copy.16 = f32[24,64,24,64]{3,2,1,0:T(8,128)} copy(f32[24,64,24,64]{3,1,2,0:T(8,128)} %scatter_fusion.2) | data formatting | bytes 18874368 | tf_op jit(solution)/shard_map/scatter-add | solution.py:38
  223.0 16.3 %reshape.146 = f32[24,64,1536,1]{2,1,0,3:T(8,128)} reshape(f32[24,64,24,64]{3,2,1,0:T(8,128)} %copy.16) | data formatting | bytes 18874368 | tf_op jit(solution)/shard_map/dot_general | solution.py:41
  239.3 9.6 %copy.17 = f32[1536,1536]{1,0:T(8,128)} copy(f32[1536,1536]{0,1:T(8,128)} %bitcast.40) | data formatting | bytes 18874368 | tf_op jit(solution)/shard_map/dot_general | solution.py:41
  249.0 95.6 %fusion = f32[24,64,24,64]{3,1,2,0:T(8,128)} fusion(f32[24,64,1536,1]{2,1,0,3:T(8,128)} %bitcast.41, f32[24,64,1536,1]{2,1,0,3:T(8,128)} %reshape.146), kind=kOutput, calls=%fused_computation.5 | convolution fusion | flops 43486543872 | bytes 28311552 | tf_op jit(solution)/shard_map/dot_general | solution.py:41
  344.5 10.8 %gather_fusion = f32[192,64,64]{2,1,0:T(8,128)} fusion(f32[24,64,24,64]{3,1,2,0:T(8,128)} %fusion, s32[192]{0:T(256)S(1)} %bitcast.39), kind=kCustom, calls=%fused_computation | custom fusion | bytes 6292992 | tf_op jit(solution)/shard_map/gather | solution.py:48
  355.4 7.0 %reshape.115 = f32[32,6,4096]{2,1,0:T(8,128)} reshape(f32[192,64,64]{2,1,0:T(8,128)} %gather_fusion) | data formatting | bytes 6291456 | tf_op jit(solution)/shard_map/reshape | solution.py:48
  362.4 101.1 %all_to_all.19 = f32[32,6,4096]{2,1,0:T(8,128)S(1)} all-to-all(f32[32,6,4096]{2,1,0:T(8,128)} %reshape.115), channel_id=1, replica_groups=mesh['pair'=32,'vir'=8] {'pair'}, dimensions={0} | all-to-all | bytes 6291456 | tf_op jit(solution)/shard_map/all_to_all | solution.py:49
  463.5 1.8 copy.18
  465.3 4.1 gather_fusion.1
  (12 shorter events, 0.7 us)
Async XLA Ops:
  6.5 232.8 %all-gather.2.cloned.1.call-start = ((), (), s32[]{:S(2)}) async-start(), calls=%async_computation.3 | async-start | bytes 10616832 | tf_op jit(solution)/shard_map/all_gather | solution.py:43
  18.7 30.9 %all-to-all-start = ((s32[32,1,6]{2,1,0:T(1,128)}), s32[32,1,6]{2,1,0:T(1,128)S(1)}, u32[]{:S(2)}, u32[]{:S(2)}) async-start(s32[32,1,6]{2,1,0:T(1,128)} %copy.14), calls=%async_computation | async-start | bytes 32768 | tf_op jit(solution)/shard_map/all_to_all | solution.py:29
  49.6 106.4 %all-to-all-start.1 = ((f32[32,6,4096]{2,1,0:T(8,128)}), f32[32,6,4096]{2,1,0:T(8,128)}, u32[]{:S(2)}, u32[]{:S(2)}) async-start(f32[32,6,4096]{2,1,0:T(8,128)} %copy.15), calls=%async_computation.1 | async-start | bytes 8388608 | tf_op jit(solution)/shard_map/all_to_all | solution.py:28
Sparse Core Ops, SparseCore 0:
  9.2 58.3 all-gather.1
where the time goes:
time: 478 us; the launch traced here: 476 us
  local copies, waits for them, and re-layouts  114 us (24%)
  blocking collectives  101 us (21%)
  waiting for transfers between devices  96.4 us (20%)
  matrix products  95.6 us (20%)
  other arithmetic  34.1 us (7%)
  starting transfers between devices  21.4 us (4%)
  between operations  13.5 us (3%)
    all_to_all x1, blocking collectives, per_device(): lax.all_to_all(answers, 'pair', split_axis=0, concat_axis=0, tiled=True)  101 us
    all_to_all x1, waiting for transfers between devices, per_device(): lax.all_to_all(send_tiles, 'pair', split_axis=0, concat_axis=0, tiled=True)  95.7 us
    dot_general x1, matrix products, per_device(): jnp.dot(blocked, lax.all_gather(integrals, 'vir', axis=0, tiled=True), pr...  95.6 us
    scatter-add x1, other arithmetic, per_device(): blocked = jnp.zeros((ROWSETS_DEV, TS, NS, TS), jnp.float32).at[row_block,...  31.4 us
    dot_general x2, local copies, waits for them, and re-layouts, per_device(): jnp.dot(blocked, lax.all_gather(integrals, 'vir', axis=0, tiled=True), pr...  26 us
    scatter-add x1, local copies, waits for them, and re-layouts, per_device(): blocked = jnp.zeros((ROWSETS_DEV, TS, NS, TS), jnp.float32).at[row_block,...  19.8 us
    scatter x2, local copies, waits for them, and re-layouts, per_device(): send_tiles = jnp.zeros((owner_count, capacity, TS * TS), jnp.float32).at[...  19.2 us
    all_to_all x1, starting transfers between devices, per_device(): lax.all_to_all(send_keys, 'pair', split_axis=0, concat_axis=0, tiled=True)  11.3 us
  transfers between devices with their start and end apart: 3, of which 1 were waited for; matrix products, arithmetic and copies ran while one was open for 24% of the time, Pallas kernels for 0%

commit v1 on v0

--- a/solution.py
+++ b/solution.py
@@ -28,20 +28,21 @@
         lax.all_to_all(send_tiles, "pair", split_axis=0, concat_axis=0, tiled=True),
         lax.all_to_all(send_keys, "pair", split_axis=0, concat_axis=0, tiled=True),
     )
-    arrived = recv_tiles.reshape(owner_count * capacity, TS, TS)
+    arrived = recv_tiles.reshape(owner_count * capacity, TS * TS)
     flat_keys = recv_keys.reshape(owner_count * capacity)
     row_block = flat_keys // NS
     col_block = flat_keys % NS
-    blocked = (
-        jnp.zeros((ROWSETS_DEV, TS, NS, TS), jnp.float32)
-        .at[row_block, :, col_block, :]
-        .add(arrived)
+    places = jnp.arange(ROWSETS_DEV * NS, dtype=jnp.int32)
+    chooser = (places[:, None] == flat_keys[None, :]).astype(jnp.float32)
+    stacked = jnp.dot(
+        chooser, arrived, precision=lax.Precision.HIGHEST, preferred_element_type=jnp.float32
     )
+    blocked = stacked.reshape(ROWSETS_DEV, NS, TS, TS).transpose(0, 2, 1, 3)
     blocked = blocked.reshape(ROWSETS_DEV * TS, NS * TS)
     product = jnp.dot(
         blocked,
         lax.all_gather(integrals, "vir", axis=0, tiled=True),
-        precision=lax.Precision.HIGHEST,
+        precision=lax.Precision.HIGH,
         preferred_element_type=jnp.float32,
     )
     product = product.reshape(ROWSETS_DEV, TS, NS, TS)

time: 478 us -> 384 us (0.80)
  matrix products: 95.6 us -> 62.5 us
  other arithmetic: 34.1 us -> 3.3 us
  local copies, waits for them, and re-layouts: 114 us -> 85.7 us
    dot_general x1, matrix products: 95.6 us -> 50.7 us  [per_device(): jnp.dot(blocked, lax.all_gather(integrals, 'vir', axis=0, tiled=True), pr...]
    scatter-add x1 -> x0, other arithmetic: 31.4 us -> none  [per_device(): blocked = jnp.zeros((ROWSETS_DEV, TS, NS, TS), jnp.float32).at[row_block,...]
    scatter-add x1 -> x0, local copies, waits for them, and re-layouts: 19.8 us -> none  [per_device(): blocked = jnp.zeros((ROWSETS_DEV, TS, NS, TS), jnp.float32).at[row_block,...]
    dot_general x0 -> x1, matrix products: none -> 11.8 us  [per_device(): jnp.dot(chooser, arrived, precision=lax.Precision.HIGHEST, preferred_elem...]
    broadcast_in_dim x1 -> x0, local copies, waits for them, and re-layouts: 8.96 us -> none  [per_device(): jnp.zeros((ROWSETS_DEV, TS, NS, TS), jnp.float32)]
  transfers between devices with their start and end apart: 3 -> 3, of which waited for: 1 -> 1; matrix products, arithmetic and copies ran while one was open for 24% -> 18% of each run, Pallas kernels for 0% -> 0%
where the time goes in v1:
time: 384 us; the launch traced here: 383 us
  blocking collectives  101 us (26%)
  waiting for transfers between devices  95.3 us (25%)
  local copies, waits for them, and re-layouts  85.7 us (22%)
  matrix products  62.5 us (16%)
  starting transfers between devices  21.2 us (6%)
  between operations  13.5 us (4%)
    all_to_all x1, blocking collectives, per_device(): lax.all_to_all(answers, 'pair', split_axis=0, concat_axis=0, tiled=True)  101 us
    all_to_all x1, waiting for transfers between devices, per_device(): lax.all_to_all(send_tiles, 'pair', split_axis=0, concat_axis=0, tiled=True)  94.6 us
    dot_general x1, matrix products, per_device(): jnp.dot(blocked, lax.all_gather(integrals, 'vir', axis=0, tiled=True), pr...  50.7 us
    dot_general x2, local copies, waits for them, and re-layouts, per_device(): jnp.dot(blocked, lax.all_gather(integrals, 'vir', axis=0, tiled=True), pr...  26 us
    scatter x2, local copies, waits for them, and re-layouts, per_device(): send_tiles = jnp.zeros((owner_count, capacity, TS * TS), jnp.float32).at[...  19.3 us
    dot_general x1, matrix products, per_device(): jnp.dot(chooser, arrived, precision=lax.Precision.HIGHEST, preferred_elem...  11.8 us
    all_to_all x1, starting transfers between devices, per_device(): lax.all_to_all(send_keys, 'pair', split_axis=0, concat_axis=0, tiled=True)  11.3 us
    gather x1, local copies, waits for them, and re-layouts, per_device(): product[row_block, :, col_block, :].reshape(owner_count, capacity, TS * TS)  10.8 us
  transfers between devices with their start and end apart: 3, of which 1 were waited for; matrix products, arithmetic and copies ran while one was open for 18% of the time, Pallas kernels for 0%

profile of v1, /device:TPU:16, one launch (start us, length us, event | category | flops | bytes accessed | tf_op | source)
XLA Modules:
  0.0 382.6 jit_solution(3705608537904763732)
XLA Ops:
  6.5 0.7 all-gather.2.cloned.1.call-update
  7.3 0.7 fusion.6
  8.1 0.8 select_reduce_fusion
  9.0 0.7 fusion.15
  9.7 8.3 %scatter_fusion = s32[32,6]{0,1:T(8,128)S(1)} fusion(s32[32,6]{0,1:T(8,128)S(1)} %broadcast_in_dim.6, s32[96]{0:T(128)S(1)} %get-tuple-element.9, s32[96]{0:T(128)} %param.7), kind=kCustom, calls=%fused_computation.2 | custom fusion | bytes 1920 | tf_op jit(solution)/shard_map/scatter | solution.py:25
  18.0 0.7 copy.15
  18.7 11.3 %all-to-all-start = ((s32[32,1,6]{2,1,0:T(1,128)}), s32[32,1,6]{2,1,0:T(1,128)S(1)}, u32[]{:S(2)}, u32[]{:S(2)}) async-start(s32[32,1,6]{2,1,0:T(1,128)} %copy.15), calls=%async_computation | async-start | bytes 32768 | tf_op jit(solution)/shard_map/all_to_all | solution.py:29
  30.4 15.4 %scatter_fusion.1 = f32[32,6,4096]{2,0,1:T(8,128)S(1)} fusion(f32[32,6,4096]{2,0,1:T(8,128)S(1)} %broadcast_in_dim.8, s32[96]{0:T(128)S(1)} %get-tuple-element.9, f32[96,4096]{1,0:T(8,128)} %param.4), kind=kCustom, calls=%fused_computation.3 | custom fusion | bytes 4719360 | tf_op jit(solution)/shard_map/scatter | solution.py:22
  45.8 3.9 %copy.16 = f32[32,6,4096]{2,1,0:T(8,128)} copy(f32[32,6,4096]{2,0,1:T(8,128)S(1)} %scatter_fusion.1) | data formatting | bytes 6291456 | tf_op jit(solution)/shard_map/scatter | solution.py:22
  49.7 9.9 %all-to-all-start.1 = ((f32[32,6,4096]{2,1,0:T(8,128)}), f32[32,6,4096]{2,1,0:T(8,128)}, u32[]{:S(2)}, u32[]{:S(2)}) async-start(f32[32,6,4096]{2,1,0:T(8,128)} %copy.16), calls=%async_computation.1 | async-start | bytes 8388608 | tf_op jit(solution)/shard_map/all_to_all | solution.py:28
  59.8 0.5 broadcast.270
  60.3 0.8 divide_reduce_fusion
  61.5 94.6 %all-to-all-done.1 = f32[32,6,4096]{2,1,0:T(8,128)} async-done(((f32[32,6,4096]{2,1,0:T(8,128)}), f32[32,6,4096]{2,1,0:T(8,128)}, u32[]{:S(2)}, u32[]{:S(2)}) %all-to-all-start.1) | async-done | bytes 3145760 | tf_op jit(solution)/shard_map/all_to_all | solution.py:28
  156.1 3.0 reshape.136
  159.1 3.3 copy.17
  162.4 11.8 %convolution_bitcast_fusion = f32[24,64,24,64]{3,2,1,0:T(8,128)} fusion(f32[64,64,192,1]{2,1,0,3:T(8,128)} %bitcast.51, s32[192]{0:T(256)S(1)} %eq.48, s32[24,24]{1,0:T(8,128)S(1)} %multiply_add_fusion), kind=kOutput, calls=%fused_computation.6 | convolution fusion | flops 5435928576 | bytes 12585984 | tf_op jit(solution)/shard_map/dot_general | solution.py:37
  174.2 16.3 %reshape.164 = f32[24,64,1536,1]{2,1,0,3:T(8,128)} reshape(f32[24,64,24,64]{3,2,1,0:T(8,128)} %convolution_bitcast_fusion) | data formatting | bytes 18874368 | tf_op jit(solution)/shard_map/dot_general | solution.py:42
  190.6 9.7 %copy.18 = f32[1536,1536]{1,0:T(8,128)} copy(f32[1536,1536]{0,1:T(8,128)} %bitcast.54) | data formatting | bytes 18874368 | tf_op jit(solution)/shard_map/dot_general | solution.py:42
  200.2 50.7 %fusion = f32[24,64,24,64]{3,1,2,0:T(8,128)} fusion(f32[24,64,1536,1]{2,1,0,3:T(8,128)} %bitcast.55, f32[24,64,1536,1]{2,1,0,3:T(8,128)} %reshape.164), kind=kOutput, calls=%fused_computation.4 | convolution fusion | flops 21743271936 | bytes 28311552 | tf_op jit(solution)/shard_map/dot_general | solution.py:42
  250.9 10.8 %gather_fusion = f32[192,64,64]{2,1,0:T(8,128)} fusion(f32[24,64,24,64]{3,1,2,0:T(8,128)} %fusion, s32[192]{0:T(256)S(1)} %bitcast.53), kind=kCustom, calls=%fused_computation | custom fusion | bytes 6292992 | tf_op jit(solution)/shard_map/gather | solution.py:49
  261.6 7.1 %reshape.137 = f32[32,6,4096]{2,1,0:T(8,128)} reshape(f32[192,64,64]{2,1,0:T(8,128)} %gather_fusion) | data formatting | bytes 6291456 | tf_op jit(solution)/shard_map/reshape | solution.py:49
  268.7 101.1 %all_to_all.19 = f32[32,6,4096]{2,1,0:T(8,128)S(1)} all-to-all(f32[32,6,4096]{2,1,0:T(8,128)} %reshape.137), channel_id=1, replica_groups=mesh['pair'=32,'vir'=8] {'pair'}, dimensions={0} | all-to-all | bytes 6291456 | tf_op jit(solution)/shard_map/all_to_all | solution.py:50
  369.8 1.8 copy.19
  371.7 4.1 %gather_fusion.1 = f32[96,4096]{1,0:T(8,128)} fusion(f32[32,6,4096]{2,0,1:T(8,128)S(1)} %copy.19, s32[96]{0:T(128)S(1)} %get-tuple-element.8), kind=kCustom, calls=%fused_computation.1 | custom fusion | bytes 3146496 | tf_op jit(solution)/shard_map/gather | solution.py:51
  (13 shorter events, 1.0 us)
Async XLA Ops:
  6.5 184.0 %all-gather.2.cloned.1.call-start = ((), (), s32[]{:S(2)}) async-start(), calls=%async_computation.3 | async-start | bytes 10616832 | tf_op jit(solution)/shard_map/all_gather | solution.py:44
  18.7 31.0 %all-to-all-start = ((s32[32,1,6]{2,1,0:T(1,128)}), s32[32,1,6]{2,1,0:T(1,128)S(1)}, u32[]{:S(2)}, u32[]{:S(2)}) async-start(s32[32,1,6]{2,1,0:T(1,128)} %copy.15), calls=%async_computation | async-start | bytes 32768 | tf_op jit(solution)/shard_map/all_to_all | solution.py:29
  49.7 106.4 %all-to-all-start.1 = ((f32[32,6,4096]{2,1,0:T(8,128)}), f32[32,6,4096]{2,1,0:T(8,128)}, u32[]{:S(2)}, u32[]{:S(2)}) async-start(f32[32,6,4096]{2,1,0:T(8,128)} %copy.16), calls=%async_computation.1 | async-start | bytes 8388608 | tf_op jit(solution)/shard_map/all_to_all | solution.py:28
Sparse Core Ops, SparseCore 0:
  9.2 58.3 all-gather.1

commit v2 on v1

--- a/solution.py
+++ b/solution.py
@@ -16,20 +16,17 @@
     )
     before = jnp.cumsum(picked, axis=0) - picked
     slot_index = jnp.sum(before * picked, axis=1)
-    send_tiles = (
-        jnp.zeros((owner_count, capacity, TS * TS), jnp.float32)
-        .at[tile_owner, slot_index]
-        .set(amplitudes)
-    )
-    send_keys = (
-        jnp.zeros((owner_count, capacity), jnp.int32).at[tile_owner, slot_index].set(tile_key)
-    )
-    recv_tiles, recv_keys = (
-        lax.all_to_all(send_tiles, "pair", split_axis=0, concat_axis=0, tiled=True),
-        lax.all_to_all(send_keys, "pair", split_axis=0, concat_axis=0, tiled=True),
-    )
-    arrived = recv_tiles.reshape(owner_count * capacity, TS * TS)
-    flat_keys = recv_keys.reshape(owner_count * capacity)
+    slots = jnp.arange(owner_count * capacity, dtype=jnp.int32)
+    packer = (slots[:, None] == (tile_owner * capacity + slot_index)[None, :]).astype(jnp.float32)
+    key_lanes = jnp.broadcast_to(tile_key.astype(jnp.float32)[:, None], (tile_key.shape[0], 128))
+    payload = jnp.concatenate([amplitudes, key_lanes], axis=1)
+    send = jnp.dot(
+        packer, payload, precision=lax.Precision.HIGHEST, preferred_element_type=jnp.float32
+    ).reshape(owner_count, capacity, TS * TS + 128)
+    recv = lax.all_to_all(send, "pair", split_axis=0, concat_axis=0, tiled=True)
+    recv = recv.reshape(owner_count * capacity, TS * TS + 128)
+    arrived = recv[:, : TS * TS]
+    flat_keys = recv[:, TS * TS].astype(jnp.int32)
     row_block = flat_keys // NS
     col_block = flat_keys % NS
     places = jnp.arange(ROWSETS_DEV * NS, dtype=jnp.int32)
@@ -48,7 +45,10 @@
     product = product.reshape(ROWSETS_DEV, TS, NS, TS)
     answers = product[row_block, :, col_block, :].reshape(owner_count, capacity, TS * TS)
     returned = lax.all_to_all(answers, "pair", split_axis=0, concat_axis=0, tiled=True)
-    return returned[tile_owner, slot_index]
+    returned = returned.reshape(owner_count * capacity, TS * TS)
+    return jnp.dot(
+        packer.T, returned, precision=lax.Precision.HIGHEST, preferred_element_type=jnp.float32
+    )
 
 
 def solution(mesh):

time: 384 us -> 380 us (0.990)
  blocking collectives: 101 us -> 211 us
  waiting for transfers between devices: 95.3 us -> 0.73 us
  starting transfers between devices: 21.2 us -> 0.01 us
    all_to_all x0 -> x1, blocking collectives: none -> 112 us  [per_device(): recv = lax.all_to_all(send, 'pair', split_axis=0, concat_axis=0, tiled=True)]
    all_to_all x2 -> x0, waiting for transfers between devices: 94.6 us -> none  [the longest x1 94.6 us: per_device(): lax.all_to_all(send_tiles, 'pair', split_axis=0, concat_axis=0, tiled=True)]
    scatter x3 -> x0, local copies, waits for them, and re-layouts: 27.6 us -> none  [the longest x2 19.3 us: per_device(): send_tiles = jnp.zeros((owner_count, capacity, TS * TS), jnp.float32).at[...]
    all_to_all x2 -> x0, starting transfers between devices: 21.2 us -> none  [the longest x1 11.3 us: per_device(): lax.all_to_all(send_keys, 'pair', split_axis=0, concat_axis=0, tiled=True)]
    reshape x1 -> x4, local copies, waits for them, and re-layouts: 3.02 us -> 24 us  [the longest x1 15.6 us: per_device(): blocked = stacked.reshape(ROWSETS_DEV, NS, TS, TS).transpose(0, 2, 1, 3)]
    transpose x0 -> x1, local copies, waits for them, and re-layouts: none -> 19.8 us  [per_device(): blocked = stacked.reshape(ROWSETS_DEV, NS, TS, TS).transpose(0, 2, 1, 3)]
    dot_general x1, matrix products: 11.8 us -> 6.29 us  [per_device(): jnp.dot(chooser, arrived, precision=lax.Precision.HIGHEST, preferred_elem...]
    dot_general x0 -> x2, matrix products: none -> 5.3 us  [the longest x1 2.85 us: per_device(): jnp.dot(packer, payload, precision=lax.Precision.HIGHEST, preferred_eleme...]
  transfers between devices with their start and end apart: 3 -> 1, of which waited for: 1 -> 0; matrix products, arithmetic and copies ran while one was open for 18% -> 18% of each run, Pallas kernels for 0% -> 0%
where the time goes in v2:
time: 380 us; the launch traced here: 378 us
  blocking collectives  211 us (56%)
  local copies, waits for them, and re-layouts  87.8 us (23%)
  matrix products  62.2 us (16%)
  between operations  13.5 us (4%)
    all_to_all x1, blocking collectives, per_device(): recv = lax.all_to_all(send, 'pair', split_axis=0, concat_axis=0, tiled=True)  112 us
    all_to_all x1, blocking collectives, per_device(): lax.all_to_all(answers, 'pair', split_axis=0, concat_axis=0, tiled=True)  99.4 us
    dot_general x1, matrix products, per_device(): jnp.dot(blocked, lax.all_gather(integrals, 'vir', axis=0, tiled=True), pr...  50.6 us
    dot_general x2, local copies, waits for them, and re-layouts, per_device(): jnp.dot(blocked, lax.all_gather(integrals, 'vir', axis=0, tiled=True), pr...  26 us
    transpose x1, local copies, waits for them, and re-layouts, per_device(): blocked = stacked.reshape(ROWSETS_DEV, NS, TS, TS).transpose(0, 2, 1, 3)  19.8 us
    reshape x1, local copies, waits for them, and re-layouts, per_device(): blocked = stacked.reshape(ROWSETS_DEV, NS, TS, TS).transpose(0, 2, 1, 3)  15.6 us
    gather x1, local copies, waits for them, and re-layouts, per_device(): product[row_block, :, col_block, :].reshape(owner_count, capacity, TS * TS)  10.8 us
  transfers between devices with their start and end apart: 1, of which 0 were waited for; matrix products, arithmetic and copies ran while one was open for 18% of the time, Pallas kernels for 0%

profile of v2, /device:TPU:16, one launch (start us, length us, event | category | flops | bytes accessed | tf_op | source)
XLA Modules:
  0.0 378.5 jit_solution(839913734201172895)
XLA Ops:
  6.5 0.7 all-gather.2.cloned.1.call-update
  7.3 0.7 convert_element_type.21
  7.9 0.7 fusion.12
  8.7 0.1 reduce_window_sum.11
  8.8 0.8 select_reduce_fusion
  9.6 0.7 multiply_add_fusion
  10.3 0.1 broadcast_in_dim.2
  10.4 2.8 fusion.4
  13.2 2.3 reshape.29
  15.6 111.8 %all_to_all.10 = f32[32,6,4224]{2,1,0:T(8,128)} all-to-all(f32[32,6,4224]{2,1,0:T(8,128)} %reshape.29), channel_id=1, replica_groups=mesh['pair'=32,'vir'=8] {'pair'}, dimensions={0} | all-to-all | bytes 6488064 | tf_op jit(solution)/shard_map/all_to_all | solution.py:26
  127.4 3.1 reshape.30
  130.4 0.1 copy.13
  130.5 6.3 %fusion.2 = f32[576,4096]{1,0:T(8,128)} fusion(f32[192,4224]{1,0:T(8,128)S(1)} %reshape.30, s32[192]{0:T(256)S(1)} %bitcast.18), kind=kOutput, calls=%fused_computation.3 | convolution fusion | flops 5435928576 | bytes 12583936 | tf_op jit(solution)/shard_map/dot_general | solution.py:34
  136.8 15.6 %reshape.31 = f32[24,24,64,64]{3,2,1,0:T(8,128)} reshape(f32[576,4096]{1,0:T(8,128)} %fusion.2) | data formatting | bytes 18874368 | tf_op jit(solution)/shard_map/reshape | solution.py:37
  152.4 19.8 %copy.10 = f32[24,64,24,64]{3,2,1,0:T(8,128)} copy(f32[24,64,24,64]{3,1,2,0:T(8,128)} %bitcast.14) | data formatting | bytes 18874368 | tf_op jit(solution)/shard_map/transpose | solution.py:37
  172.2 16.3 %reshape.40 = f32[24,64,1536,1]{2,1,0,3:T(8,128)} reshape(f32[24,64,24,64]{3,2,1,0:T(8,128)} %copy.10) | data formatting | bytes 18874368 | tf_op jit(solution)/shard_map/dot_general | solution.py:39
  188.5 0.0 all-gather.2.cloned.1.call-done
  188.6 9.7 %copy.11 = f32[1536,1536]{1,0:T(8,128)} copy(f32[1536,1536]{0,1:T(8,128)} %bitcast.16) | data formatting | bytes 18874368 | tf_op jit(solution)/shard_map/dot_general | solution.py:39
  198.2 50.6 %fusion = f32[24,64,24,64]{3,1,2,0:T(8,128)} fusion(f32[24,64,1536,1]{2,1,0,3:T(8,128)} %bitcast.17, f32[24,64,1536,1]{2,1,0,3:T(8,128)} %reshape.40), kind=kOutput, calls=%fused_computation.1 | convolution fusion | flops 21743271936 | bytes 28311552 | tf_op jit(solution)/shard_map/dot_general | solution.py:39
  248.9 10.8 %gather_fusion = f32[192,64,64]{2,1,0:T(8,128)} fusion(f32[24,64,24,64]{3,1,2,0:T(8,128)} %fusion, s32[192]{0:T(256)S(1)} %bitcast.15), kind=kCustom, calls=%fused_computation | custom fusion | bytes 6292992 | tf_op jit(solution)/shard_map/gather | solution.py:46
  259.7 7.0 %reshape.32 = f32[32,6,4096]{2,1,0:T(8,128)} reshape(f32[192,64,64]{2,1,0:T(8,128)} %gather_fusion) | data formatting | bytes 6291456 | tf_op jit(solution)/shard_map/reshape | solution.py:46
  266.7 99.4 %all_to_all.11 = f32[32,6,4096]{2,1,0:T(8,128)} all-to-all(f32[32,6,4096]{2,1,0:T(8,128)} %reshape.32), channel_id=1, replica_groups=mesh['pair'=32,'vir'=8] {'pair'}, dimensions={0} | all-to-all | bytes 6291456 | tf_op jit(solution)/shard_map/all_to_all | solution.py:47
  366.1 3.0 reshape.33
  369.2 2.5 fusion.9
  (4 shorter events, 0.0 us)
Async XLA Ops:
  6.5 182.0 %all-gather.2.cloned.1.call-start = ((), (), s32[]{:S(2)}) async-start(), calls=%async_computation.2 | async-start | bytes 10616832 | tf_op jit(solution)/shard_map/all_gather | solution.py:41
Sparse Core Ops, SparseCore 0:
  9.2 58.3 all-gather.1

commit v3 on v2

--- a/solution.py
+++ b/solution.py
@@ -8,25 +8,30 @@
 ROWSETS_DEV = 24
 
 
+def slots_of(owners, count):
+    picked = (owners[..., :, None] == jnp.arange(count, dtype=jnp.int32)).astype(jnp.int32)
+    before = jnp.cumsum(picked, axis=-2) - picked
+    return jnp.sum(before * picked, axis=-1)
+
+
 def per_device(amplitudes, integrals, tile_owner, tile_key):
     owner_count = lax.axis_size("pair")
     capacity = max(2, 2 * amplitudes.shape[0] // owner_count)
-    picked = (tile_owner[:, None] == jnp.arange(owner_count, dtype=jnp.int32)[None, :]).astype(
-        jnp.int32
-    )
-    before = jnp.cumsum(picked, axis=0) - picked
-    slot_index = jnp.sum(before * picked, axis=1)
+    slot_index = slots_of(tile_owner, owner_count)
+    owners_all = lax.all_gather(tile_owner, "pair", axis=0)
+    keys_all = lax.all_gather(tile_key, "pair", axis=0)
+    me = lax.axis_index("pair")
+    slots_all = slots_of(owners_all, owner_count)
+    mine = owners_all == me
+    hits = mine[:, :, None] & (slots_all[:, :, None] == jnp.arange(capacity, dtype=jnp.int32))
+    flat_keys = jnp.sum(jnp.where(hits, keys_all[:, :, None], 0), axis=1).reshape(-1)
     slots = jnp.arange(owner_count * capacity, dtype=jnp.int32)
     packer = (slots[:, None] == (tile_owner * capacity + slot_index)[None, :]).astype(jnp.float32)
-    key_lanes = jnp.broadcast_to(tile_key.astype(jnp.float32)[:, None], (tile_key.shape[0], 128))
-    payload = jnp.concatenate([amplitudes, key_lanes], axis=1)
     send = jnp.dot(
-        packer, payload, precision=lax.Precision.HIGHEST, preferred_element_type=jnp.float32
-    ).reshape(owner_count, capacity, TS * TS + 128)
+        packer, amplitudes, precision=lax.Precision.HIGHEST, preferred_element_type=jnp.float32
+    ).reshape(owner_count, capacity, TS * TS)
     recv = lax.all_to_all(send, "pair", split_axis=0, concat_axis=0, tiled=True)
-    recv = recv.reshape(owner_count * capacity, TS * TS + 128)
-    arrived = recv[:, : TS * TS]
-    flat_keys = recv[:, TS * TS].astype(jnp.int32)
+    arrived = recv.reshape(owner_count * capacity, TS * TS)
     row_block = flat_keys // NS
     col_block = flat_keys % NS
     places = jnp.arange(ROWSETS_DEV * NS, dtype=jnp.int32)

time: 380 us -> 465 us (1.22)
  blocking collectives: 211 us -> 297 us
  local copies, waits for them, and re-layouts: 87.8 us -> 65 us
  starting transfers between devices: 0.01 us -> 11.6 us
  matrix products: 62.2 us -> 69.9 us
    unnamed x0 -> x1, blocking collectives: none -> 223 us
    all_to_all x1 -> x0, blocking collectives: 112 us -> none  [per_device(): recv = lax.all_to_all(send, 'pair', split_axis=0, concat_axis=0, tiled=True)]
    all_to_all x1, blocking collectives: 99.4 us -> 74.1 us  [per_device(): lax.all_to_all(answers, 'pair', split_axis=0, concat_axis=0, tiled=True)]
    transpose x1 -> x0, local copies, waits for them, and re-layouts: 19.8 us -> none  [per_device(): blocked = stacked.reshape(ROWSETS_DEV, NS, TS, TS).transpose(0, 2, 1, 3)]
    reshape x3 -> x2, local copies, waits for them, and re-layouts: 21 us -> 9 us  [the longest x1 4.7 us: per_device(): arrived = recv.reshape(owner_count * capacity, TS * TS)]
    all_to_all x0 -> x1, starting transfers between devices: none -> 11.6 us  [per_device(): recv = lax.all_to_all(send, 'pair', split_axis=0, concat_axis=0, tiled=True)]
    dot_general x1, matrix products: 6.29 us -> 11.8 us  [per_device(): jnp.dot(chooser, arrived, precision=lax.Precision.HIGHEST, preferred_elem...]
    dot_general x0 -> x1, local copies, waits for them, and re-layouts: none -> 5.11 us  [per_device(): jnp.dot(chooser, arrived, precision=lax.Precision.HIGHEST, preferred_elem...]
  transfers between devices with their start and end apart: 1 -> 2, of which waited for: 0 -> 0; matrix products, arithmetic and copies ran while one was open for 18% -> 11% of each run, Pallas kernels for 0% -> 0%
where the time goes in v3:
time: 465 us; the launch traced here: 463 us
  blocking collectives  297 us (64%)
  matrix products  69.9 us (15%)
  local copies, waits for them, and re-layouts  65 us (14%)
  between operations  14.2 us (3%)
  starting transfers between devices  11.6 us (2%)
  other arithmetic  5.13 us (1%)
    unnamed x1, blocking collectives  223 us
    all_to_all x1, blocking collectives, per_device(): lax.all_to_all(answers, 'pair', split_axis=0, concat_axis=0, tiled=True)  74.1 us
    dot_general x1, matrix products, per_device(): jnp.dot(blocked, lax.all_gather(integrals, 'vir', axis=0, tiled=True), pr...  50.7 us
    dot_general x2, local copies, waits for them, and re-layouts, per_device(): jnp.dot(blocked, lax.all_gather(integrals, 'vir', axis=0, tiled=True), pr...  26 us
    dot_general x1, matrix products, per_device(): jnp.dot(chooser, arrived, precision=lax.Precision.HIGHEST, preferred_elem...  11.8 us
    all_to_all x1, starting transfers between devices, per_device(): recv = lax.all_to_all(send, 'pair', split_axis=0, concat_axis=0, tiled=True)  11.6 us
    gather x1, local copies, waits for them, and re-layouts, per_device(): product[row_block, :, col_block, :].reshape(owner_count, capacity, TS * TS)  10.8 us
  transfers between devices with their start and end apart: 2, of which 0 were waited for; matrix products, arithmetic and copies ran while one was open for 11% of the time, Pallas kernels for 0%

profile of v3, /device:TPU:16, one launch (start us, length us, event | category | flops | bytes accessed | tf_op | source)
XLA Modules:
  0.0 463.5 jit_solution(11038985649045765247)
XLA Ops:
  6.5 0.7 all-gather.4.cloned.1.call-update
  7.3 0.7 fusion.17
  8.1 0.8 select_reduce_fusion.1
  9.0 0.7 multiply_add_fusion.1
  9.6 3.1 fusion.13
  12.7 4.3 reshape.129
  17.0 11.6 %all-to-all-start = ((f32[32,6,4096]{2,1,0:T(8,128)}), f32[32,6,4096]{2,1,0:T(8,128)}, u32[]{:S(2)}, u32[]{:S(2)}) async-start(f32[32,6,4096]{2,1,0:T(8,128)} %reshape.129), calls=%async_computation | async-start | bytes 8388608 | tf_op jit(solution)/shard_map/all_to_all | solution.py:33
  28.6 0.6 dynamic-slice
  29.9 0.3 dynamic-update-slice
  30.2 0.3 dynamic-update-slice.1
  30.5 223.0 %all-reduce.2 = (s32[3072]{0:T(1024)S(1)}, s32[3072]{0:T(1024)S(1)}) all-reduce(s32[3072]{0:T(1024)S(1)} %dynamic-update-slice.1, s32[3072]{0:T(1024)S(1)} %dynamic-update-slice), channel_id=3, replica_groups=mesh['pair'=32,'vir'=8] {'pair'}, use_global_device_ids=true, to_apply=%add.1 | all-reduce | flops 6144 | bytes 49152
  253.6 2.5 fusion.23
  256.3 0.2 select_reduce_fusion
  257.3 4.7 %reshape.130 = f32[192,4096]{1,0:T(8,128)} reshape(f32[32,6,4096]{2,1,0:T(8,128)} %all-to-all-done) | data formatting | bytes 6291456 | tf_op jit(solution)/shard_map/reshape | solution.py:34
  262.0 5.1 %copy.18 = f32[4096,192]{1,0:T(8,128)} copy(f32[4096,192]{0,1:T(8,128)} %bitcast.27) | data formatting | bytes 6291456 | tf_op jit(solution)/shard_map/dot_general | solution.py:39
  267.1 11.8 %convolution_bitcast_fusion = f32[24,64,24,64]{3,2,1,0:T(8,128)} fusion(f32[64,64,192,1]{2,1,0,3:T(8,128)} %bitcast.26, s32[192]{0:T(256)S(1)} %eq.104, s32[24,24]{1,0:T(8,128)S(1)} %multiply_add_fusion), kind=kOutput, calls=%fused_computation.3 | convolution fusion | flops 5435928576 | bytes 12585984 | tf_op jit(solution)/shard_map/dot_general | solution.py:39
  279.0 16.3 %reshape.153 = f32[24,64,1536,1]{2,1,0,3:T(8,128)} reshape(f32[24,64,24,64]{3,2,1,0:T(8,128)} %convolution_bitcast_fusion) | data formatting | bytes 18874368 | tf_op jit(solution)/shard_map/dot_general | solution.py:44
  295.3 9.7 %copy.19 = f32[1536,1536]{1,0:T(8,128)} copy(f32[1536,1536]{0,1:T(8,128)} %bitcast.29) | data formatting | bytes 18874368 | tf_op jit(solution)/shard_map/dot_general | solution.py:44
  305.0 50.7 %fusion = f32[24,64,24,64]{3,1,2,0:T(8,128)} fusion(f32[24,64,1536,1]{2,1,0,3:T(8,128)} %bitcast.30, f32[24,64,1536,1]{2,1,0,3:T(8,128)} %reshape.153), kind=kOutput, calls=%fused_computation.1 | convolution fusion | flops 21743271936 | bytes 28311552 | tf_op jit(solution)/shard_map/dot_general | solution.py:44
  355.6 10.8 %gather_fusion = f32[192,64,64]{2,1,0:T(8,128)} fusion(f32[24,64,24,64]{3,1,2,0:T(8,128)} %fusion, s32[192]{0:T(256)S(1)} %bitcast.28), kind=kCustom, calls=%fused_computation | custom fusion | bytes 6292992 | tf_op jit(solution)/shard_map/gather | solution.py:51
  366.4 7.1 %reshape.131 = f32[32,6,4096]{2,1,0:T(8,128)} reshape(f32[192,64,64]{2,1,0:T(8,128)} %gather_fusion) | data formatting | bytes 6291456 | tf_op jit(solution)/shard_map/reshape | solution.py:51
  373.4 74.1 %all_to_all.10 = f32[32,6,4096]{2,1,0:T(8,128)} all-to-all(f32[32,6,4096]{2,1,0:T(8,128)} %reshape.131), channel_id=1, replica_groups=mesh['pair'=32,'vir'=8] {'pair'}, dimensions={0} | all-to-all | bytes 6291456 | tf_op jit(solution)/shard_map/all_to_all | solution.py:52
  447.5 4.8 %reshape.132 = f32[192,4096]{1,0:T(8,128)} reshape(f32[32,6,4096]{2,1,0:T(8,128)} %all_to_all.10) | data formatting | bytes 6291456 | tf_op jit(solution)/shard_map/reshape | solution.py:53
  452.3 4.3 fusion.12
  (33 shorter events, 1.3 us)
Async XLA Ops:
  6.5 3.1 copy-start
  6.5 288.8 %all-gather.4.cloned.1.call-start = ((), (), s32[]{:S(2)}) async-start(), calls=%async_computation.2 | async-start | bytes 10616832 | tf_op jit(solution)/shard_map/all_gather | solution.py:46
  17.0 11.6 %copy-start.4 = (u32[256]{0:T(256)S(1)}, u32[256]{0:T(256)}, u32[]{:S(2)}) copy-start(u32[256]{0:T(256)} %constant.58) | copy-start | bytes 3076
  17.0 12.9 %copy-start.2 = (s32[96]{0:T(128)S(1)}, s32[96]{0:T(128)}, u32[]{:S(2)}) copy-start(s32[96]{0:T(128)} %param.6) | copy-start | bytes 1156
  17.0 13.1 %copy-start.3 = (s32[96]{0:T(128)S(1)}, s32[96]{0:T(128)}, u32[]{:S(2)}) copy-start(s32[96]{0:T(128)} %param.7) | copy-start | bytes 1156
  17.0 240.3 %all-to-all-start = ((f32[32,6,4096]{2,1,0:T(8,128)}), f32[32,6,4096]{2,1,0:T(8,128)}, u32[]{:S(2)}, u32[]{:S(2)}) async-start(f32[32,6,4096]{2,1,0:T(8,128)} %reshape.129), calls=%async_computation | async-start | bytes 8388608 | tf_op jit(solution)/shard_map/all_to_all | solution.py:33
  447.5 9.1 %copy-start.1 = (f32[96,4096]{1,0:T(8,128)S(1)}, f32[96,4096]{1,0:T(8,128)}, u32[]{:S(2)}) copy-start(f32[96,4096]{1,0:T(8,128)} %param.4) | copy-start | bytes 4718596
Sparse Core Ops, SparseCore 0:
  9.2 58.3 all-gather.3

commit v4 on v2

--- a/solution.py
+++ b/solution.py
@@ -18,15 +18,16 @@
     slot_index = jnp.sum(before * picked, axis=1)
     slots = jnp.arange(owner_count * capacity, dtype=jnp.int32)
     packer = (slots[:, None] == (tile_owner * capacity + slot_index)[None, :]).astype(jnp.float32)
-    key_lanes = jnp.broadcast_to(tile_key.astype(jnp.float32)[:, None], (tile_key.shape[0], 128))
-    payload = jnp.concatenate([amplitudes, key_lanes], axis=1)
     send = jnp.dot(
-        packer, payload, precision=lax.Precision.HIGHEST, preferred_element_type=jnp.float32
-    ).reshape(owner_count, capacity, TS * TS + 128)
+        packer, amplitudes, precision=lax.Precision.HIGHEST, preferred_element_type=jnp.float32
+    ).reshape(owner_count, capacity, TS * TS)
+    send_keys = (
+        jnp.zeros((owner_count, capacity), jnp.int32).at[tile_owner, slot_index].set(tile_key)
+    )
     recv = lax.all_to_all(send, "pair", split_axis=0, concat_axis=0, tiled=True)
-    recv = recv.reshape(owner_count * capacity, TS * TS + 128)
-    arrived = recv[:, : TS * TS]
-    flat_keys = recv[:, TS * TS].astype(jnp.int32)
+    recv_keys = lax.all_to_all(send_keys, "pair", split_axis=0, concat_axis=0, tiled=True)
+    arrived = recv.reshape(owner_count * capacity, TS * TS)
+    flat_keys = recv_keys.reshape(owner_count * capacity)
     row_block = flat_keys // NS
     col_block = flat_keys % NS
     places = jnp.arange(ROWSETS_DEV * NS, dtype=jnp.int32)

time: 380 us -> 379 us (level)
  blocking collectives: 211 us -> 101 us
  waiting for transfers between devices: 0.73 us -> 97 us
  starting transfers between devices: 0.01 us -> 19.6 us
  local copies, waits for them, and re-layouts: 87.8 us -> 72.8 us
  matrix products: 62.2 us -> 69.9 us
    all_to_all x1 -> x0, blocking collectives: 112 us -> none  [per_device(): recv = lax.all_to_all(send, 'pair', split_axis=0, concat_axis=0, tiled=True)]
    all_to_all x0 -> x2, waiting for transfers between devices: none -> 96.2 us  [the longest x1 94.6 us: per_device(): recv = lax.all_to_all(send, 'pair', split_axis=0, concat_axis=0, tiled=True)]
    transpose x1 -> x0, local copies, waits for them, and re-layouts: 19.8 us -> none  [per_device(): blocked = stacked.reshape(ROWSETS_DEV, NS, TS, TS).transpose(0, 2, 1, 3)]
    all_to_all x0 -> x2, starting transfers between devices: none -> 19.6 us  [the longest x1 11.3 us: per_device(): lax.all_to_all(send_keys, 'pair', split_axis=0, concat_axis=0, tiled=True)]
    reshape x3 -> x2, local copies, waits for them, and re-layouts: 21 us -> 9.05 us  [the longest x1 4.69 us: per_device(): arrived = recv.reshape(owner_count * capacity, TS * TS)]
    scatter x0 -> x1, local copies, waits for them, and re-layouts: none -> 8.34 us  [per_device(): jnp.zeros((owner_count, capacity), jnp.int32).at[tile_owner, slot_index]]
    dot_general x1, matrix products: 6.29 us -> 11.8 us  [per_device(): jnp.dot(chooser, arrived, precision=lax.Precision.HIGHEST, preferred_elem...]
    dot_general x0 -> x1, local copies, waits for them, and re-layouts: none -> 5.11 us  [per_device(): jnp.dot(chooser, arrived, precision=lax.Precision.HIGHEST, preferred_elem...]
  transfers between devices with their start and end apart: 1 -> 3, of which waited for: 0 -> 2; matrix products, arithmetic and copies ran while one was open for 18% -> 16% of each run, Pallas kernels for 0% -> 0%
where the time goes in v4:
time: 379 us; the launch traced here: 378 us
  blocking collectives  101 us (27%)
  waiting for transfers between devices  97 us (26%)
  local copies, waits for them, and re-layouts  72.8 us (19%)
  matrix products  69.9 us (18%)
  starting transfers between devices  19.6 us (5%)
  between operations  13.5 us (4%)
  other arithmetic  3.96 us (1%)
    all_to_all x1, blocking collectives, per_device(): lax.all_to_all(answers, 'pair', split_axis=0, concat_axis=0, tiled=True)  101 us
    all_to_all x1, waiting for transfers between devices, per_device(): recv = lax.all_to_all(send, 'pair', split_axis=0, concat_axis=0, tiled=True)  94.6 us
    dot_general x1, matrix products, per_device(): jnp.dot(blocked, lax.all_gather(integrals, 'vir', axis=0, tiled=True), pr...  50.7 us
    dot_general x2, local copies, waits for them, and re-layouts, per_device(): jnp.dot(blocked, lax.all_gather(integrals, 'vir', axis=0, tiled=True), pr...  26 us
    dot_general x1, matrix products, per_device(): jnp.dot(chooser, arrived, precision=lax.Precision.HIGHEST, preferred_elem...  11.8 us
    all_to_all x1, starting transfers between devices, per_device(): lax.all_to_all(send_keys, 'pair', split_axis=0, concat_axis=0, tiled=True)  11.3 us
    gather x1, local copies, waits for them, and re-layouts, per_device(): product[row_block, :, col_block, :].reshape(owner_count, capacity, TS * TS)  10.8 us
    scatter x1, local copies, waits for them, and re-layouts, per_device(): jnp.zeros((owner_count, capacity), jnp.int32).at[tile_owner, slot_index]  8.34 us
  transfers between devices with their start and end apart: 3, of which 2 were waited for; matrix products, arithmetic and copies ran while one was open for 16% of the time, Pallas kernels for 0%

profile of v4, /device:TPU:16, one launch (start us, length us, event | category | flops | bytes accessed | tf_op | source)
XLA Modules:
  0.0 377.8 jit_solution(9110378785625981087)
XLA Ops:
  6.5 0.7 all-gather.2.cloned.1.call-update
  7.3 0.7 fusion.10
  8.1 0.8 select_reduce_fusion
  9.0 0.7 fusion.18
  9.7 8.3 %scatter_fusion = s32[32,6]{0,1:T(8,128)S(1)} fusion(s32[32,6]{0,1:T(8,128)S(1)} %broadcast_in_dim.4, s32[96]{0:T(128)S(1)} %fusion.18, s32[96]{0:T(128)} %param.7), kind=kCustom, calls=%fused_computation.1 | custom fusion | bytes 1920 | tf_op jit(solution)/shard_map/scatter | solution.py:25
  18.0 0.7 copy.13
  18.7 11.3 %all-to-all-start = ((s32[32,1,6]{2,1,0:T(1,128)}), s32[32,1,6]{2,1,0:T(1,128)S(1)}, u32[]{:S(2)}, u32[]{:S(2)}) async-start(s32[32,1,6]{2,1,0:T(1,128)} %copy.13), calls=%async_computation | async-start | bytes 32768 | tf_op jit(solution)/shard_map/all_to_all | solution.py:28
  30.7 3.1 fusion.7
  33.8 4.4 %reshape.143 = f32[32,6,4096]{2,1,0:T(8,128)} reshape(f32[192,4096]{1,0:T(8,128)} %fusion.7) | data formatting | bytes 6291456 | tf_op jit(solution)/shard_map/reshape | solution.py:23
  38.1 1.6 all-to-all-done
  39.8 8.3 %all-to-all-start.1 = ((f32[32,6,4096]{2,1,0:T(8,128)}), f32[32,6,4096]{2,1,0:T(8,128)}, u32[]{:S(2)}, u32[]{:S(2)}) async-start(f32[32,6,4096]{2,1,0:T(8,128)} %reshape.143), calls=%async_computation.1 | async-start | bytes 8388608 | tf_op jit(solution)/shard_map/all_to_all | solution.py:27
  48.8 0.8 divide_reduce_fusion
  49.9 94.6 %all-to-all-done.1 = f32[32,6,4096]{2,1,0:T(8,128)} async-done(((f32[32,6,4096]{2,1,0:T(8,128)}), f32[32,6,4096]{2,1,0:T(8,128)}, u32[]{:S(2)}, u32[]{:S(2)}) %all-to-all-start.1) | async-done | bytes 3145760 | tf_op jit(solution)/shard_map/all_to_all | solution.py:27
  144.6 4.7 %reshape.144 = f32[192,4096]{1,0:T(8,128)} reshape(f32[32,6,4096]{2,1,0:T(8,128)} %all-to-all-done.1) | data formatting | bytes 6291456 | tf_op jit(solution)/shard_map/reshape | solution.py:29
  149.3 5.1 %copy.14 = f32[4096,192]{1,0:T(8,128)} copy(f32[4096,192]{0,1:T(8,128)} %bitcast.41) | data formatting | bytes 6291456 | tf_op jit(solution)/shard_map/dot_general | solution.py:35
  154.4 11.8 %convolution_bitcast_fusion = f32[24,64,24,64]{3,2,1,0:T(8,128)} fusion(f32[64,64,192,1]{2,1,0,3:T(8,128)} %bitcast.40, s32[192]{0:T(256)S(1)} %eq.64, s32[24,24]{1,0:T(8,128)S(1)} %multiply_add_fusion), kind=kOutput, calls=%fused_computation.4 | convolution fusion | flops 5435928576 | bytes 12585984 | tf_op jit(solution)/shard_map/dot_general | solution.py:35
  166.2 16.3 %reshape.161 = f32[24,64,1536,1]{2,1,0,3:T(8,128)} reshape(f32[24,64,24,64]{3,2,1,0:T(8,128)} %convolution_bitcast_fusion) | data formatting | bytes 18874368 | tf_op jit(solution)/shard_map/dot_general | solution.py:40
  182.5 9.7 %copy.15 = f32[1536,1536]{1,0:T(8,128)} copy(f32[1536,1536]{0,1:T(8,128)} %bitcast.43) | data formatting | bytes 18874368 | tf_op jit(solution)/shard_map/dot_general | solution.py:40
  192.2 50.7 %fusion = f32[24,64,24,64]{3,1,2,0:T(8,128)} fusion(f32[24,64,1536,1]{2,1,0,3:T(8,128)} %bitcast.44, f32[24,64,1536,1]{2,1,0,3:T(8,128)} %reshape.161), kind=kOutput, calls=%fused_computation.2 | convolution fusion | flops 21743271936 | bytes 28311552 | tf_op jit(solution)/shard_map/dot_general | solution.py:40
  242.8 10.8 %gather_fusion = f32[192,64,64]{2,1,0:T(8,128)} fusion(f32[24,64,24,64]{3,1,2,0:T(8,128)} %fusion, s32[192]{0:T(256)S(1)} %bitcast.42), kind=kCustom, calls=%fused_computation | custom fusion | bytes 6292992 | tf_op jit(solution)/shard_map/gather | solution.py:47
  253.6 7.1 %reshape.145 = f32[32,6,4096]{2,1,0:T(8,128)} reshape(f32[192,64,64]{2,1,0:T(8,128)} %gather_fusion) | data formatting | bytes 6291456 | tf_op jit(solution)/shard_map/reshape | solution.py:47
  260.7 101.2 %all_to_all.19 = f32[32,6,4096]{2,1,0:T(8,128)} all-to-all(f32[32,6,4096]{2,1,0:T(8,128)} %reshape.145), channel_id=1, replica_groups=mesh['pair'=32,'vir'=8] {'pair'}, dimensions={0} | all-to-all | bytes 6291456 | tf_op jit(solution)/shard_map/all_to_all | solution.py:48
  361.9 4.8 %reshape.146 = f32[192,4096]{1,0:T(8,128)} reshape(f32[32,6,4096]{2,1,0:T(8,128)} %all_to_all.19) | data formatting | bytes 6291456 | tf_op jit(solution)/shard_map/reshape | solution.py:49
  366.7 4.3 %fusion.6 = f32[96,4096]{1,0:T(8,128)} fusion(f32[192,4096]{1,0:T(8,128)} %reshape.146, s32[96]{0:T(128)S(1)} %multiply_add_fusion.1), kind=kOutput, calls=%fused_computation.10 | convolution fusion | flops 905988096 | bytes 4718976 | tf_op jit(solution)/shard_map/dot_general | solution.py:50
  (17 shorter events, 1.8 us)
Async XLA Ops:
  6.5 24.1 %copy-start = (f32[96,4096]{1,0:T(8,128)S(1)}, f32[96,4096]{1,0:T(8,128)}, u32[]{:S(2)}) copy-start(f32[96,4096]{1,0:T(8,128)} %param.4) | copy-start | bytes 4718596
  6.5 176.0 %all-gather.2.cloned.1.call-start = ((), (), s32[]{:S(2)}) async-start(), calls=%async_computation.3 | async-start | bytes 10616832 | tf_op jit(solution)/shard_map/all_gather | solution.py:42
  18.7 21.1 %all-to-all-start = ((s32[32,1,6]{2,1,0:T(1,128)}), s32[32,1,6]{2,1,0:T(1,128)S(1)}, u32[]{:S(2)}, u32[]{:S(2)}) async-start(s32[32,1,6]{2,1,0:T(1,128)} %copy.13), calls=%async_computation | async-start | bytes 32768 | tf_op jit(solution)/shard_map/all_to_all | solution.py:28
  39.8 104.8 %all-to-all-start.1 = ((f32[32,6,4096]{2,1,0:T(8,128)}), f32[32,6,4096]{2,1,0:T(8,128)}, u32[]{:S(2)}, u32[]{:S(2)}) async-start(f32[32,6,4096]{2,1,0:T(8,128)} %reshape.143), calls=%async_computation.1 | async-start | bytes 8388608 | tf_op jit(solution)/shard_map/all_to_all | solution.py:27
  361.9 9.1 %copy-start.1 = (f32[96,4096]{1,0:T(8,128)S(1)}, f32[96,4096]{1,0:T(8,128)}, u32[]{:S(2)}) copy-start(f32[96,4096]{1,0:T(8,128)} %param.4) | copy-start | bytes 4718596
Sparse Core Ops, SparseCore 0:
  9.2 58.3 all-gather.1

commit v5 on v4

--- a/solution.py
+++ b/solution.py
@@ -43,8 +43,10 @@
         precision=lax.Precision.HIGH,
         preferred_element_type=jnp.float32,
     )
-    product = product.reshape(ROWSETS_DEV, TS, NS, TS)
-    answers = product[row_block, :, col_block, :].reshape(owner_count, capacity, TS * TS)
+    pairs = product.reshape(ROWSETS_DEV, TS, NS // 2, 2 * TS)[row_block, :, col_block // 2, :]
+    answers = jnp.where(
+        (col_block % 2 == 0)[:, None, None], pairs[:, :, :TS], pairs[:, :, TS:]
+    ).reshape(owner_count, capacity, TS * TS)
     returned = lax.all_to_all(answers, "pair", split_axis=0, concat_axis=0, tiled=True)
     returned = returned.reshape(owner_count * capacity, TS * TS)
     return jnp.dot(

time: 379 us -> 363 us (0.958)
  matrix products: 69.9 us -> 47.8 us
  other arithmetic: 3.96 us -> 12.5 us
    dot_general x1, matrix products: 50.7 us -> 28.6 us  [per_device(): jnp.dot(blocked, lax.all_gather(integrals, 'vir', axis=0, tiled=True), pr...]
    select_n x0 -> x1, other arithmetic: none -> 8.48 us  [per_device(): jnp.where((col_block % 2 == 0)[:, None, None], pairs[:, :, :TS], pairs[:,...]
where the time goes in v5:
time: 363 us; the launch traced here: 362 us
  blocking collectives  101 us (28%)
  waiting for transfers between devices  96.7 us (27%)
  local copies, waits for them, and re-layouts  70 us (19%)
  matrix products  47.8 us (13%)
  starting transfers between devices  19.8 us (5%)
  between operations  13.5 us (4%)
  other arithmetic  12.5 us (3%)
    all_to_all x1, blocking collectives, per_device(): lax.all_to_all(answers, 'pair', split_axis=0, concat_axis=0, tiled=True)  101 us
    all_to_all x1, waiting for transfers between devices, per_device(): recv = lax.all_to_all(send, 'pair', split_axis=0, concat_axis=0, tiled=True)  94.4 us
    dot_general x1, matrix products, per_device(): jnp.dot(blocked, lax.all_gather(integrals, 'vir', axis=0, tiled=True), pr...  28.6 us
    dot_general x2, local copies, waits for them, and re-layouts, per_device(): jnp.dot(blocked, lax.all_gather(integrals, 'vir', axis=0, tiled=True), pr...  26 us
    dot_general x1, matrix products, per_device(): jnp.dot(chooser, arrived, precision=lax.Precision.HIGHEST, preferred_elem...  11.8 us
    all_to_all x1, starting transfers between devices, per_device(): lax.all_to_all(send_keys, 'pair', split_axis=0, concat_axis=0, tiled=True)  11.3 us
    select_n x1, other arithmetic, per_device(): jnp.where((col_block % 2 == 0)[:, None, None], pairs[:, :, :TS], pairs[:,...  8.48 us
    all_to_all x1, starting transfers between devices, per_device(): recv = lax.all_to_all(send, 'pair', split_axis=0, concat_axis=0, tiled=True)  8.48 us
  transfers between devices with their start and end apart: 3, of which 2 were waited for; matrix products, arithmetic and copies ran while one was open for 16% of the time, Pallas kernels for 0%

profile of v5, /device:TPU:16, one launch (start us, length us, event | category | flops | bytes accessed | tf_op | source)
XLA Modules:
  0.0 361.7 jit_solution(16678402661491145241)
XLA Ops:
  6.5 0.7 all-gather.2.cloned.1.call-update
  7.3 0.7 fusion.10
  8.1 0.8 select_reduce_fusion
  9.7 8.3 %scatter_fusion = s32[32,6]{0,1:T(8,128)S(1)} fusion(s32[32,6]{0,1:T(8,128)S(1)} %broadcast_in_dim.9, s32[96]{0:T(128)S(1)} %fusion.20, s32[96]{0:T(128)} %param.7), kind=kCustom, calls=%fused_computation.1 | custom fusion | bytes 1920 | tf_op jit(solution)/shard_map/scatter | solution.py:25
  18.0 0.7 copy.13
  18.7 11.3 %all-to-all-start = ((s32[32,1,6]{2,1,0:T(1,128)}), s32[32,1,6]{2,1,0:T(1,128)S(1)}, u32[]{:S(2)}, u32[]{:S(2)}) async-start(s32[32,1,6]{2,1,0:T(1,128)} %copy.13), calls=%async_computation | async-start | bytes 32768 | tf_op jit(solution)/shard_map/all_to_all | solution.py:28
  30.7 3.1 fusion.7
  33.8 4.4 %reshape.214 = f32[32,6,4096]{2,1,0:T(8,128)} reshape(f32[192,4096]{1,0:T(8,128)} %fusion.7) | data formatting | bytes 6291456 | tf_op jit(solution)/shard_map/reshape | solution.py:23
  38.1 1.6 all-to-all-done
  39.8 8.5 %all-to-all-start.1 = ((f32[32,6,4096]{2,1,0:T(8,128)}), f32[32,6,4096]{2,1,0:T(8,128)}, u32[]{:S(2)}, u32[]{:S(2)}) async-start(f32[32,6,4096]{2,1,0:T(8,128)} %reshape.214), calls=%async_computation.1 | async-start | bytes 8388608 | tf_op jit(solution)/shard_map/all_to_all | solution.py:27
  48.8 0.8 divide_reduce_fusion
  50.2 94.4 %all-to-all-done.1 = f32[32,6,4096]{2,1,0:T(8,128)} async-done(((f32[32,6,4096]{2,1,0:T(8,128)}), f32[32,6,4096]{2,1,0:T(8,128)}, u32[]{:S(2)}, u32[]{:S(2)}) %all-to-all-start.1) | async-done | bytes 3145760 | tf_op jit(solution)/shard_map/all_to_all | solution.py:27
  144.5 4.7 %reshape.215 = f32[192,4096]{1,0:T(8,128)} reshape(f32[32,6,4096]{2,1,0:T(8,128)} %all-to-all-done.1) | data formatting | bytes 6291456 | tf_op jit(solution)/shard_map/reshape | solution.py:29
  149.2 5.1 %copy.14 = f32[4096,192]{1,0:T(8,128)} copy(f32[4096,192]{0,1:T(8,128)} %bitcast.40) | data formatting | bytes 6291456 | tf_op jit(solution)/shard_map/dot_general | solution.py:35
  154.3 11.8 %convolution_bitcast_fusion = f32[24,64,24,64]{3,2,1,0:T(8,128)} fusion(f32[64,64,192,1]{2,1,0,3:T(8,128)} %bitcast.39, s32[192]{0:T(256)S(1)} %reshape.213, s32[24,24]{1,0:T(8,128)S(1)} %multiply_add_fusion), kind=kOutput, calls=%fused_computation.4 | convolution fusion | flops 5435928576 | bytes 12585984 | tf_op jit(solution)/shard_map/dot_general | solution.py:35
  166.2 16.3 %reshape.232 = f32[24,64,1536,1]{2,1,0,3:T(8,128)} reshape(f32[24,64,24,64]{3,2,1,0:T(8,128)} %convolution_bitcast_fusion) | data formatting | bytes 18874368 | tf_op jit(solution)/shard_map/dot_general | solution.py:40
  182.5 9.6 %copy.15 = f32[1536,1536]{1,0:T(8,128)} copy(f32[1536,1536]{0,1:T(8,128)} %bitcast.42) | data formatting | bytes 18874368 | tf_op jit(solution)/shard_map/dot_general | solution.py:40
  192.1 28.6 %fusion = f32[24,64,12,128]{3,1,2,0:T(8,128)} fusion(f32[12,128,1536,1]{2,1,0,3:T(8,128)} %bitcast.43, f32[24,64,1536,1]{2,1,0,3:T(8,128)} %reshape.232), kind=kOutput, calls=%fused_computation.2 | convolution fusion | flops 21743271936 | bytes 28311552 | tf_op jit(solution)/shard_map/dot_general | solution.py:40
  220.7 8.2 %gather_fusion = f32[192,64,128]{2,1,0:T(8,128)} fusion(f32[24,64,12,128]{3,1,2,0:T(8,128)} %fusion, s32[192]{0:T(256)S(1)} %bitcast.41), kind=kCustom, calls=%fused_computation | custom fusion | bytes 12584448 | tf_op jit(solution)/shard_map/gather | solution.py:46
  228.9 8.5 %slice_select_fusion = f32[192,64,64]{2,1,0:T(8,128)} fusion(f32[192,64,128]{2,1,0:T(8,128)} %gather_fusion, pred[192]{0:T(512)(128)(4,1)S(1)} %fusion.17), kind=kLoop, calls=%fused_computation.5 | loop fusion | flops 786432 | bytes 9437376 | tf_op jit(solution)/shard_map/jit(_where)/select_n | solution.py:47
  237.4 7.1 %reshape.216 = f32[32,6,4096]{2,1,0:T(8,128)} reshape(f32[192,64,64]{2,1,0:T(8,128)} %slice_select_fusion) | data formatting | bytes 6291456 | tf_op jit(solution)/shard_map/reshape | solution.py:49
  244.4 101.4 %all_to_all.19 = f32[32,6,4096]{2,1,0:T(8,128)} all-to-all(f32[32,6,4096]{2,1,0:T(8,128)} %reshape.216), channel_id=1, replica_groups=mesh['pair'=32,'vir'=8] {'pair'}, dimensions={0} | all-to-all | bytes 6291456 | tf_op jit(solution)/shard_map/all_to_all | solution.py:50
  345.8 4.7 %reshape.217 = f32[192,4096]{1,0:T(8,128)} reshape(f32[32,6,4096]{2,1,0:T(8,128)} %all_to_all.19) | data formatting | bytes 6291456 | tf_op jit(solution)/shard_map/reshape | solution.py:51
  350.5 4.3 %fusion.6 = f32[96,4096]{1,0:T(8,128)} fusion(f32[192,4096]{1,0:T(8,128)} %reshape.217, s32[96]{0:T(128)S(1)} %multiply_add_fusion.1), kind=kOutput, calls=%fused_computation.11 | convolution fusion | flops 905988096 | bytes 4718976 | tf_op jit(solution)/shard_map/dot_general | solution.py:52
  (19 shorter events, 2.6 us)
Async XLA Ops:
  6.5 24.1 %copy-start = (f32[96,4096]{1,0:T(8,128)S(1)}, f32[96,4096]{1,0:T(8,128)}, u32[]{:S(2)}) copy-start(f32[96,4096]{1,0:T(8,128)} %param.4) | copy-start | bytes 4718596
  6.5 176.0 %all-gather.2.cloned.1.call-start = ((), (), s32[]{:S(2)}) async-start(), calls=%async_computation.3 | async-start | bytes 10616832 | tf_op jit(solution)/shard_map/all_gather | solution.py:42
  18.7 21.1 %all-to-all-start = ((s32[32,1,6]{2,1,0:T(1,128)}), s32[32,1,6]{2,1,0:T(1,128)S(1)}, u32[]{:S(2)}, u32[]{:S(2)}) async-start(s32[32,1,6]{2,1,0:T(1,128)} %copy.13), calls=%async_computation | async-start | bytes 32768 | tf_op jit(solution)/shard_map/all_to_all | solution.py:28
  39.8 104.8 %all-to-all-start.1 = ((f32[32,6,4096]{2,1,0:T(8,128)}), f32[32,6,4096]{2,1,0:T(8,128)}, u32[]{:S(2)}, u32[]{:S(2)}) async-start(f32[32,6,4096]{2,1,0:T(8,128)} %reshape.214), calls=%async_computation.1 | async-start | bytes 8388608 | tf_op jit(solution)/shard_map/all_to_all | solution.py:27
  244.4 110.4 %copy-start.1 = (f32[96,4096]{1,0:T(8,128)S(1)}, f32[96,4096]{1,0:T(8,128)}, u32[]{:S(2)}) copy-start(f32[96,4096]{1,0:T(8,128)} %param.4) | copy-start | bytes 4718596
Sparse Core Ops, SparseCore 0:
  9.2 58.3 all-gather.1

commit v6 on v5

--- a/solution.py
+++ b/solution.py
@@ -30,16 +30,25 @@
     flat_keys = recv_keys.reshape(owner_count * capacity)
     row_block = flat_keys // NS
     col_block = flat_keys % NS
-    places = jnp.arange(ROWSETS_DEV * NS, dtype=jnp.int32)
-    chooser = (places[:, None] == flat_keys[None, :]).astype(jnp.float32)
+    tiles = arrived.reshape(owner_count * capacity, TS, TS)
+    empty = jnp.zeros_like(tiles)
+    odd = (col_block % 2 == 1)[:, None, None]
+    halves = jnp.concatenate(
+        [jnp.where(odd, empty, tiles), jnp.where(odd, tiles, empty)], axis=2
+    ).reshape(owner_count * capacity, TS * 2 * TS)
+    places = jnp.arange(ROWSETS_DEV * NS // 2, dtype=jnp.int32)
+    chooser = (places[:, None] == (row_block * (NS // 2) + col_block // 2)[None, :]).astype(
+        jnp.float32
+    )
     stacked = jnp.dot(
-        chooser, arrived, precision=lax.Precision.HIGHEST, preferred_element_type=jnp.float32
+        chooser, halves, precision=lax.Precision.HIGHEST, preferred_element_type=jnp.float32
     )
-    blocked = stacked.reshape(ROWSETS_DEV, NS, TS, TS).transpose(0, 2, 1, 3)
-    blocked = blocked.reshape(ROWSETS_DEV * TS, NS * TS)
-    product = jnp.dot(
+    blocked = stacked.reshape(ROWSETS_DEV, NS // 2, TS, 2 * TS).transpose(0, 2, 1, 3)
+    right = lax.all_gather(integrals, "vir", axis=0, tiled=True).reshape(NS // 2, 2 * TS, NS * TS)
+    product = lax.dot_general(
         blocked,
-        lax.all_gather(integrals, "vir", axis=0, tiled=True),
+        right,
+        (((2, 3), (0, 1)), ((), ())),
         precision=lax.Precision.HIGH,
         preferred_element_type=jnp.float32,
     )

time: 363 us -> 362 us (level)
  local copies, waits for them, and re-layouts: 70 us -> 50.9 us
  other arithmetic: 12.5 us -> 22.1 us
  matrix products: 47.8 us -> 56.8 us
    dot_general x3 -> x1, local copies, waits for them, and re-layouts: 31.1 us -> 9.66 us  [per_device(): lax.dot_general(blocked, right, (((2, 3), (0, 1)), ((), ())), precision=l...]
    dot_general x2, matrix products: 40.4 us -> 49.4 us  [the longest x1 36.1 us: per_device(): lax.dot_general(blocked, right, (((2, 3), (0, 1)), ((), ())), precision=l...]
    another operation x0 -> x1, local copies, waits for them, and re-layouts: none -> 6.83 us  [per_device(): tiles = arrived.reshape(owner_count * capacity, TS, TS)]
    select_n x0 -> x1, other arithmetic: none -> 5.17 us  [per_device(): jnp.where(odd, empty, tiles)]
    reshape x2 -> x0, local copies, waits for them, and re-layouts: 4.8 us -> none  [the longest x1 4.69 us: per_device(): arrived = recv.reshape(owner_count * capacity, TS * TS)]
    concatenate x0 -> x1, other arithmetic: none -> 4.47 us  [per_device(): jnp.concatenate([jnp.where(odd, empty, tiles), jnp.where(odd, tiles, empt...]
  transfers between devices with their start and end apart: 3 -> 3, of which waited for: 2 -> 2; matrix products, arithmetic and copies ran while one was open for 16% -> 14% of each run, Pallas kernels for 0% -> 0%
where the time goes in v6:
time: 362 us; the launch traced here: 361 us
  blocking collectives  101 us (28%)
  waiting for transfers between devices  96.5 us (27%)
  matrix products  56.8 us (16%)
  local copies, waits for them, and re-layouts  50.9 us (14%)
  other arithmetic  22.1 us (6%)
  starting transfers between devices  19.8 us (5%)
  between operations  13.5 us (4%)
    all_to_all x1, blocking collectives, per_device(): lax.all_to_all(answers, 'pair', split_axis=0, concat_axis=0, tiled=True)  101 us
    all_to_all x1, waiting for transfers between devices, per_device(): recv = lax.all_to_all(send, 'pair', split_axis=0, concat_axis=0, tiled=True)  94.2 us
    dot_general x1, matrix products, per_device(): lax.dot_general(blocked, right, (((2, 3), (0, 1)), ((), ())), precision=l...  36.1 us
    dot_general x1, matrix products, per_device(): jnp.dot(chooser, halves, precision=lax.Precision.HIGHEST, preferred_eleme...  13.3 us
    all_to_all x1, starting transfers between devices, per_device(): lax.all_to_all(send_keys, 'pair', split_axis=0, concat_axis=0, tiled=True)  11.3 us
    dot_general x1, local copies, waits for them, and re-layouts, per_device(): lax.dot_general(blocked, right, (((2, 3), (0, 1)), ((), ())), precision=l...  9.66 us
    all_to_all x1, starting transfers between devices, per_device(): recv = lax.all_to_all(send, 'pair', split_axis=0, concat_axis=0, tiled=True)  8.49 us
    select_n x1, other arithmetic, per_device(): jnp.where((col_block % 2 == 0)[:, None, None], pairs[:, :, :TS], pairs[:,...  8.48 us
  transfers between devices with their start and end apart: 3, of which 2 were waited for; matrix products, arithmetic and copies ran while one was open for 14% of the time, Pallas kernels for 0%

profile of v6, /device:TPU:16, one launch (start us, length us, event | category | flops | bytes accessed | tf_op | source)
XLA Modules:
  0.0 361.0 jit_solution(9940554781041243553)
XLA Ops:
  6.5 0.7 all-gather.2.cloned.1.call-update
  7.3 0.7 fusion.20
  8.1 0.8 select_reduce_fusion
  9.7 8.3 %scatter_fusion = s32[32,6]{0,1:T(8,128)S(1)} fusion(s32[32,6]{0,1:T(8,128)S(1)} %broadcast_in_dim.36, s32[96]{0:T(128)S(1)} %fusion.30, s32[96]{0:T(128)} %param.7), kind=kCustom, calls=%fused_computation.1 | custom fusion | bytes 1920 | tf_op jit(solution)/shard_map/scatter | solution.py:25
  18.0 0.7 copy.31
  18.7 11.3 %all-to-all-start = ((s32[32,1,6]{2,1,0:T(1,128)}), s32[32,1,6]{2,1,0:T(1,128)S(1)}, u32[]{:S(2)}, u32[]{:S(2)}) async-start(s32[32,1,6]{2,1,0:T(1,128)} %copy.31), calls=%async_computation | async-start | bytes 32768 | tf_op jit(solution)/shard_map/all_to_all | solution.py:28
  30.7 3.1 fusion.17
  33.8 4.4 %reshape.261 = f32[32,6,4096]{2,1,0:T(8,128)} reshape(f32[192,4096]{1,0:T(8,128)} %fusion.17) | data formatting | bytes 6291456 | tf_op jit(solution)/shard_map/reshape | solution.py:23
  38.1 1.6 all-to-all-done
  39.8 8.5 %all-to-all-start.1 = ((f32[32,6,4096]{2,1,0:T(8,128)}), f32[32,6,4096]{2,1,0:T(8,128)}, u32[]{:S(2)}, u32[]{:S(2)}) async-start(f32[32,6,4096]{2,1,0:T(8,128)} %reshape.261), calls=%async_computation.1 | async-start | bytes 8388608 | tf_op jit(solution)/shard_map/all_to_all | solution.py:27
  49.1 0.8 broadcast_remainder_fusion
  50.4 94.2 %all-to-all-done.1 = f32[32,6,4096]{2,1,0:T(8,128)} async-done(((f32[32,6,4096]{2,1,0:T(8,128)}), f32[32,6,4096]{2,1,0:T(8,128)}, u32[]{:S(2)}, u32[]{:S(2)}) %all-to-all-start.1) | async-done | bytes 3145760 | tf_op jit(solution)/shard_map/all_to_all | solution.py:27
  144.5 6.8 %reshape_reshape.3 = f32[192,64,64]{2,1,0:T(8,128)} reshape(f32[32,6,4096]{2,1,0:T(8,128)} %all-to-all-done.1) | data formatting | bytes 6291456 | tf_op jit(solution)/shard_map/reshape;reshape | solution.py:33
  151.4 5.2 %broadcast_select_fusion.1 = (f32[192,64,64]{2,1,0:T(8,128)S(1)}, f32[192,64,64]{2,1,0:T(8,128)}) fusion(f32[192,64,64]{2,1,0:T(8,128)} %reshape_reshape.3, pred[192]{0:T(512)(128)(4,1)S(1)} %broadcast_compare_fusion), kind=kLoop, calls=%fused_computation.15 | loop fusion | flops 1572864 | bytes 9437376 | tf_op jit(solution)/shard_map/jit(_where)/select_n | solution.py:37
  156.5 4.5 %pad_maximum_fusion = f32[192,64,128]{2,1,0:T(8,128)S(1)} fusion(f32[192,64,64]{2,1,0:T(8,128)} %get-tuple-element.10, f32[192,64,64]{2,1,0:T(8,128)S(1)} %get-tuple-element.9), kind=kLoop, calls=%fused_computation.11 | loop fusion | flops 1572864 | bytes 12582912 | tf_op jit(solution)/shard_map/concatenate | solution.py:36
  161.0 13.3 %fusion.6 = f32[24,64,12,128,1]{3,2,1,0,4:T(8,128)} fusion(s32[192]{0:T(256)S(1)} %fusion.22, s32[24,12]{1,0:T(8,128)S(1)} %multiply_add_fusion, f32[24,8,64,128]{3,2,1,0:T(8,128)S(1)} %bitcast.61), kind=kOutput, calls=%fused_computation.12 | convolution fusion | flops 5435873280 | bytes 15730560 | tf_op jit(solution)/shard_map/dot_general | solution.py:43
  174.3 9.7 %copy.33 = f32[1536,12,128]{2,0,1:T(8,128)} copy(f32[1536,12,128]{0,2,1:T(8,128)} %bitcast.63) | data formatting | bytes 18874368 | tf_op jit(solution)/shard_map/dot_general | solution.py:48
  184.0 36.1 %fusion.7 = f32[24,64,12,128]{3,1,2,0:T(8,128)} fusion(f32[12,128,12,128]{3,1,0,2:T(8,128)} %bitcast.64, f32[24,64,12,128,1]{3,2,1,0,4:T(8,128)} %fusion.6), kind=kOutput, calls=%fused_computation.13 | convolution fusion | flops 21743271936 | bytes 28311552 | tf_op jit(solution)/shard_map/dot_general | solution.py:48
  220.1 8.2 %gather_fusion = f32[192,64,128]{2,1,0:T(8,128)} fusion(f32[24,64,12,128]{3,1,2,0:T(8,128)} %fusion.7, s32[192]{0:T(256)S(1)} %bitcast.62), kind=kCustom, calls=%fused_computation | custom fusion | bytes 12584448 | tf_op jit(solution)/shard_map/gather | solution.py:55
  228.2 8.5 %slice_select_fusion = f32[192,64,64]{2,1,0:T(8,128)} fusion(f32[192,64,128]{2,1,0:T(8,128)} %gather_fusion, pred[192]{0:T(512)(128)(4,1)S(1)} %get-tuple-element.5), kind=kLoop, calls=%fused_computation.10 | loop fusion | flops 786432 | bytes 9437376 | tf_op jit(solution)/shard_map/jit(_where)/select_n | solution.py:56
  236.7 7.1 %reshape.264 = f32[32,6,4096]{2,1,0:T(8,128)} reshape(f32[192,64,64]{2,1,0:T(8,128)} %slice_select_fusion) | data formatting | bytes 6291456 | tf_op jit(solution)/shard_map/reshape | solution.py:58
  243.8 101.4 %all_to_all.19 = f32[32,6,4096]{2,1,0:T(8,128)} all-to-all(f32[32,6,4096]{2,1,0:T(8,128)} %reshape.264), channel_id=1, replica_groups=mesh['pair'=32,'vir'=8] {'pair'}, dimensions={0} | all-to-all | bytes 6291456 | tf_op jit(solution)/shard_map/all_to_all | solution.py:59
  345.2 4.7 %reshape.265 = f32[192,4096]{1,0:T(8,128)} reshape(f32[32,6,4096]{2,1,0:T(8,128)} %all_to_all.19) | data formatting | bytes 6291456 | tf_op jit(solution)/shard_map/reshape | solution.py:60
  349.8 4.3 %fusion.16 = f32[96,4096]{1,0:T(8,128)} fusion(f32[192,4096]{1,0:T(8,128)} %reshape.265, s32[96]{0:T(128)S(1)} %multiply_add_fusion.1), kind=kOutput, calls=%fused_computation.21 | convolution fusion | flops 905988096 | bytes 4718976 | tf_op jit(solution)/shard_map/dot_general | solution.py:61
  (23 shorter events, 2.8 us)
Async XLA Ops:
  6.5 24.1 %copy-start = (f32[96,4096]{1,0:T(8,128)S(1)}, f32[96,4096]{1,0:T(8,128)}, u32[]{:S(2)}) copy-start(f32[96,4096]{1,0:T(8,128)} %param.4) | copy-start | bytes 4718596
  6.5 167.8 %all-gather.2.cloned.1.call-start = ((), (), s32[]{:S(2)}) async-start(), calls=%async_computation.3 | async-start | bytes 10616832 | tf_op jit(solution)/shard_map/all_gather | solution.py:47
  18.7 21.1 %all-to-all-start = ((s32[32,1,6]{2,1,0:T(1,128)}), s32[32,1,6]{2,1,0:T(1,128)S(1)}, u32[]{:S(2)}, u32[]{:S(2)}) async-start(s32[32,1,6]{2,1,0:T(1,128)} %copy.31), calls=%async_computation | async-start | bytes 32768 | tf_op jit(solution)/shard_map/all_to_all | solution.py:28
  39.8 104.8 %all-to-all-start.1 = ((f32[32,6,4096]{2,1,0:T(8,128)}), f32[32,6,4096]{2,1,0:T(8,128)}, u32[]{:S(2)}, u32[]{:S(2)}) async-start(f32[32,6,4096]{2,1,0:T(8,128)} %reshape.261), calls=%async_computation.1 | async-start | bytes 8388608 | tf_op jit(solution)/shard_map/all_to_all | solution.py:27
  243.8 110.4 %copy-start.1 = (f32[96,4096]{1,0:T(8,128)S(1)}, f32[96,4096]{1,0:T(8,128)}, u32[]{:S(2)}) copy-start(f32[96,4096]{1,0:T(8,128)} %param.4) | copy-start | bytes 4718596
Sparse Core Ops, SparseCore 0:
  9.2 58.3 all-gather.1

commit v7 on v6

--- a/solution.py
+++ b/solution.py
@@ -18,16 +18,15 @@
     slot_index = jnp.sum(before * picked, axis=1)
     slots = jnp.arange(owner_count * capacity, dtype=jnp.int32)
     packer = (slots[:, None] == (tile_owner * capacity + slot_index)[None, :]).astype(jnp.float32)
+    key_lanes = jnp.broadcast_to(tile_key.astype(jnp.float32)[:, None], (tile_key.shape[0], 128))
+    payload = jnp.concatenate([amplitudes, key_lanes], axis=1)
     send = jnp.dot(
-        packer, amplitudes, precision=lax.Precision.HIGHEST, preferred_element_type=jnp.float32
-    ).reshape(owner_count, capacity, TS * TS)
-    send_keys = (
-        jnp.zeros((owner_count, capacity), jnp.int32).at[tile_owner, slot_index].set(tile_key)
-    )
+        packer, payload, precision=lax.Precision.HIGHEST, preferred_element_type=jnp.float32
+    ).reshape(owner_count, capacity, TS * TS + 128)
     recv = lax.all_to_all(send, "pair", split_axis=0, concat_axis=0, tiled=True)
-    recv_keys = lax.all_to_all(send_keys, "pair", split_axis=0, concat_axis=0, tiled=True)
-    arrived = recv.reshape(owner_count * capacity, TS * TS)
-    flat_keys = recv_keys.reshape(owner_count * capacity)
+    recv = recv.reshape(owner_count * capacity, TS * TS + 128)
+    arrived = recv[:, : TS * TS]
+    flat_keys = recv[:, TS * TS].astype(jnp.int32)
     row_block = flat_keys // NS
     col_block = flat_keys % NS
     tiles = arrived.reshape(owner_count * capacity, TS, TS)

time: 362 us -> 350 us (0.967)
  starting transfers between devices: 19.8 us -> 11.4 us
  waiting for transfers between devices: 96.5 us -> 101 us
    all_to_all x1 -> x0, starting transfers between devices: 11.3 us -> none  [per_device(): lax.all_to_all(send_keys, 'pair', split_axis=0, concat_axis=0, tiled=True)]
    reshape x1 -> x3, local copies, waits for them, and re-layouts: 4.36 us -> 14 us  [the longest x1 8.71 us: per_device(): halves = jnp.concatenate([jnp.where(odd, empty, tiles), jnp.where(odd, ti...]
    scatter x1 -> x0, local copies, waits for them, and re-layouts: 8.34 us -> none  [per_device(): jnp.zeros((owner_count, capacity), jnp.int32).at[tile_owner, slot_index]]
    slice x0 -> x3, local copies, waits for them, and re-layouts: none -> 7.17 us  [the longest x2 7.17 us: per_device(): arrived = recv[:, :TS * TS]]
    another operation x1 -> x0, local copies, waits for them, and re-layouts: 6.83 us -> none  [per_device(): tiles = arrived.reshape(owner_count * capacity, TS, TS)]
    all_to_all x1, waiting for transfers between devices: 94.2 us -> 99.8 us  [per_device(): recv = lax.all_to_all(send, 'pair', split_axis=0, concat_axis=0, tiled=True)]
  transfers between devices with their start and end apart: 3 -> 2, of which waited for: 2 -> 1; matrix products, arithmetic and copies ran while one was open for 14% -> 13% of each run, Pallas kernels for 0% -> 0%
where the time goes in v7:
time: 350 us; the launch traced here: 349 us
  blocking collectives  102 us (29%)
  waiting for transfers between devices  101 us (29%)
  matrix products  54 us (15%)
  local copies, waits for them, and re-layouts  49.2 us (14%)
  other arithmetic  18.7 us (5%)
  between operations  13.5 us (4%)
  starting transfers between devices  11.4 us (3%)
    all_to_all x1, blocking collectives, per_device(): lax.all_to_all(answers, 'pair', split_axis=0, concat_axis=0, tiled=True)  102 us
    all_to_all x1, waiting for transfers between devices, per_device(): recv = lax.all_to_all(send, 'pair', split_axis=0, concat_axis=0, tiled=True)  99.8 us
    dot_general x1, matrix products, per_device(): lax.dot_general(blocked, right, (((2, 3), (0, 1)), ((), ())), precision=l...  36.1 us
    dot_general x1, matrix products, per_device(): jnp.dot(chooser, halves, precision=lax.Precision.HIGHEST, preferred_eleme...  12.6 us
    all_to_all x1, starting transfers between devices, per_device(): recv = lax.all_to_all(send, 'pair', split_axis=0, concat_axis=0, tiled=True)  11.4 us
    dot_general x1, local copies, waits for them, and re-layouts, per_device(): lax.dot_general(blocked, right, (((2, 3), (0, 1)), ((), ())), precision=l...  9.66 us
    reshape x1, local copies, waits for them, and re-layouts, per_device(): halves = jnp.concatenate([jnp.where(odd, empty, tiles), jnp.where(odd, ti...  8.71 us
    select_n x1, other arithmetic, per_device(): jnp.where((col_block % 2 == 0)[:, None, None], pairs[:, :, :TS], pairs[:,...  8.48 us
  transfers between devices with their start and end apart: 2, of which 1 were waited for; matrix products, arithmetic and copies ran while one was open for 13% of the time, Pallas kernels for 0%

profile of v7, /device:TPU:16, one launch (start us, length us, event | category | flops | bytes accessed | tf_op | source)
XLA Modules:
  0.0 349.1 jit_solution(6858113116147479484)
XLA Ops:
  6.5 0.7 all-gather.2.cloned.1.call-update
  7.3 0.7 convert_element_type.26
  7.9 0.7 fusion.23
  8.8 0.8 select_reduce_fusion
  9.6 0.7 multiply_add_fusion.1
  10.4 2.8 fusion.12
  13.2 2.2 reshape.115
  15.5 11.4 %all-to-all-start = ((f32[32,6,4224]{2,1,0:T(8,128)}), f32[32,6,4224]{2,1,0:T(8,128)}, u32[]{:S(2)}, u32[]{:S(2)}) async-start(f32[32,6,4224]{2,1,0:T(8,128)} %reshape.115), calls=%async_computation | async-start | bytes 8650752 | tf_op jit(solution)/shard_map/all_to_all | solution.py:26
  26.9 99.8 %all-to-all-done = f32[32,6,4224]{2,1,0:T(8,128)} async-done(((f32[32,6,4224]{2,1,0:T(8,128)}), f32[32,6,4224]{2,1,0:T(8,128)}, u32[]{:S(2)}, u32[]{:S(2)}) %all-to-all-start) | async-done | bytes 3244064 | tf_op jit(solution)/shard_map/all_to_all | solution.py:26
  126.8 3.1 reshape.116
  129.8 2.0 slice.19
  131.9 5.1 %copy.18 = f32[192,4096]{0,1:T(8,128)} copy(f32[192,4096]{1,0:T(8,128)} %slice.19) | data formatting | bytes 6291456 | tf_op jit(solution)/shard_map/slice | solution.py:28
  137.1 3.2 broadcast_select_fusion.1
  140.4 3.9 %pad_maximum_fusion = f32[192,64,128]{0,2,1:T(8,128)} fusion(f32[192,64,64]{0,2,1:T(8,128)S(1)} %get-tuple-element.10, f32[192,64,64]{0,2,1:T(8,128)S(1)} %get-tuple-element.9), kind=kLoop, calls=%fused_computation.5 | loop fusion | flops 1572864 | bytes 12582912 | tf_op jit(solution)/shard_map/concatenate | solution.py:35
  144.3 8.7 %copy.19 = f32[192,8192]{1,0:T(8,128)} copy(f32[192,8192]{0,1:T(8,128)} %bitcast.42) | data formatting | bytes 12582912 | tf_op jit(solution)/shard_map/reshape | solution.py:37
  153.0 12.6 %fusion.6 = f32[24,64,12,128,1]{3,2,1,0,4:T(8,128)} fusion(s32[192]{0:T(256)S(1)} %fusion.25, s32[24,12]{1,0:T(8,128)S(1)} %multiply_add_fusion, f32[192,8192]{1,0:T(8,128)} %copy.19), kind=kOutput, calls=%fused_computation.10 | convolution fusion | flops 5435873280 | bytes 15730560 | tf_op jit(solution)/shard_map/dot_general | solution.py:42
  165.6 9.7 %copy.21 = f32[1536,12,128]{2,0,1:T(8,128)} copy(f32[1536,12,128]{0,2,1:T(8,128)} %bitcast.45) | data formatting | bytes 18874368 | tf_op jit(solution)/shard_map/dot_general | solution.py:47
  175.2 36.1 %fusion.7 = f32[24,64,12,128]{3,1,2,0:T(8,128)} fusion(f32[12,128,12,128]{3,1,0,2:T(8,128)} %bitcast.46, f32[24,64,12,128,1]{3,2,1,0,4:T(8,128)} %fusion.6), kind=kOutput, calls=%fused_computation.11 | convolution fusion | flops 21743271936 | bytes 28311552 | tf_op jit(solution)/shard_map/dot_general | solution.py:47
  211.4 8.2 %gather_fusion = f32[192,64,128]{2,1,0:T(8,128)} fusion(f32[24,64,12,128]{3,1,2,0:T(8,128)} %fusion.7, s32[192]{0:T(256)S(1)} %bitcast.44), kind=kCustom, calls=%fused_computation | custom fusion | bytes 12584448 | tf_op jit(solution)/shard_map/gather | solution.py:54
  219.5 8.5 %slice_select_fusion = f32[192,64,64]{2,1,0:T(8,128)} fusion(f32[192,64,128]{2,1,0:T(8,128)} %gather_fusion, pred[192]{0:T(512)(128)(4,1)S(1)} %get-tuple-element.5), kind=kLoop, calls=%fused_computation.9 | loop fusion | flops 786432 | bytes 9437376 | tf_op jit(solution)/shard_map/jit(_where)/select_n | solution.py:55
  228.0 7.1 %reshape.120 = f32[32,6,4096]{2,1,0:T(8,128)} reshape(f32[192,64,64]{2,1,0:T(8,128)} %slice_select_fusion) | data formatting | bytes 6291456 | tf_op jit(solution)/shard_map/reshape | solution.py:57
  235.1 101.8 %all_to_all.10 = f32[32,6,4096]{2,1,0:T(8,128)} all-to-all(f32[32,6,4096]{2,1,0:T(8,128)} %reshape.120), channel_id=1, replica_groups=mesh['pair'=32,'vir'=8] {'pair'}, dimensions={0} | all-to-all | bytes 6291456 | tf_op jit(solution)/shard_map/all_to_all | solution.py:58
  336.8 3.0 reshape.121
  339.8 2.5 fusion.20
  (12 shorter events, 0.4 us)
Async XLA Ops:
  6.5 159.0 %all-gather.2.cloned.1.call-start = ((), (), s32[]{:S(2)}) async-start(), calls=%async_computation.2 | async-start | bytes 10616832 | tf_op jit(solution)/shard_map/all_gather | solution.py:46
  15.5 111.3 %all-to-all-start = ((f32[32,6,4224]{2,1,0:T(8,128)}), f32[32,6,4224]{2,1,0:T(8,128)}, u32[]{:S(2)}, u32[]{:S(2)}) async-start(f32[32,6,4224]{2,1,0:T(8,128)} %reshape.115), calls=%async_computation | async-start | bytes 8650752 | tf_op jit(solution)/shard_map/all_to_all | solution.py:26
Sparse Core Ops, SparseCore 0:
  9.2 58.3 all-gather.1

commit v8 on v7

--- a/solution.py
+++ b/solution.py
@@ -40,7 +40,7 @@
         jnp.float32
     )
     stacked = jnp.dot(
-        chooser, halves, precision=lax.Precision.HIGHEST, preferred_element_type=jnp.float32
+        chooser, halves, precision=lax.Precision.HIGH, preferred_element_type=jnp.float32
     )
     blocked = stacked.reshape(ROWSETS_DEV, NS // 2, TS, 2 * TS).transpose(0, 2, 1, 3)
     right = lax.all_gather(integrals, "vir", axis=0, tiled=True).reshape(NS // 2, 2 * TS, NS * TS)

time: 350 us -> 347 us (level)
  no operation moved by 1% of the time
where the time goes in v8:
time: 347 us; the launch traced here: 346 us
  blocking collectives  102 us (29%)
  waiting for transfers between devices  101 us (29%)
  matrix products  51 us (15%)
  local copies, waits for them, and re-layouts  49.2 us (14%)
  other arithmetic  18.7 us (5%)
  between operations  13.5 us (4%)
  starting transfers between devices  11.4 us (3%)
    all_to_all x1, blocking collectives, per_device(): lax.all_to_all(answers, 'pair', split_axis=0, concat_axis=0, tiled=True)  102 us
    all_to_all x1, waiting for transfers between devices, per_device(): recv = lax.all_to_all(send, 'pair', split_axis=0, concat_axis=0, tiled=True)  99.8 us
    dot_general x1, matrix products, per_device(): lax.dot_general(blocked, right, (((2, 3), (0, 1)), ((), ())), precision=l...  36.1 us
    all_to_all x1, starting transfers between devices, per_device(): recv = lax.all_to_all(send, 'pair', split_axis=0, concat_axis=0, tiled=True)  11.4 us
    dot_general x1, local copies, waits for them, and re-layouts, per_device(): lax.dot_general(blocked, right, (((2, 3), (0, 1)), ((), ())), precision=l...  9.66 us
    dot_general x1, matrix products, per_device(): jnp.dot(chooser, halves, precision=lax.Precision.HIGH, preferred_element_...  9.57 us
    reshape x1, local copies, waits for them, and re-layouts, per_device(): halves = jnp.concatenate([jnp.where(odd, empty, tiles), jnp.where(odd, ti...  8.71 us
    select_n x1, other arithmetic, per_device(): jnp.where((col_block % 2 == 0)[:, None, None], pairs[:, :, :TS], pairs[:,...  8.48 us
  transfers between devices with their start and end apart: 2, of which 1 were waited for; matrix products, arithmetic and copies ran while one was open for 13% of the time, Pallas kernels for 0%

profile of v8, /device:TPU:16, one launch (start us, length us, event | category | flops | bytes accessed | tf_op | source)
XLA Modules:
  0.0 346.1 jit_solution(9379682264297514724)
XLA Ops:
  6.5 0.7 all-gather.2.cloned.1.call-update
  7.3 0.7 convert_element_type.26
  7.9 0.7 fusion.23
  8.8 0.8 select_reduce_fusion
  9.6 0.7 multiply_add_fusion.1
  10.4 2.8 fusion.12
  13.2 2.2 reshape.115
  15.5 11.4 %all-to-all-start = ((f32[32,6,4224]{2,1,0:T(8,128)}), f32[32,6,4224]{2,1,0:T(8,128)}, u32[]{:S(2)}, u32[]{:S(2)}) async-start(f32[32,6,4224]{2,1,0:T(8,128)} %reshape.115), calls=%async_computation | async-start | bytes 8650752 | tf_op jit(solution)/shard_map/all_to_all | solution.py:26
  26.9 99.8 %all-to-all-done = f32[32,6,4224]{2,1,0:T(8,128)} async-done(((f32[32,6,4224]{2,1,0:T(8,128)}), f32[32,6,4224]{2,1,0:T(8,128)}, u32[]{:S(2)}, u32[]{:S(2)}) %all-to-all-start) | async-done | bytes 3244064 | tf_op jit(solution)/shard_map/all_to_all | solution.py:26
  126.8 3.1 reshape.116
  129.8 2.0 slice.19
  131.9 5.1 %copy.18 = f32[192,4096]{0,1:T(8,128)} copy(f32[192,4096]{1,0:T(8,128)} %slice.19) | data formatting | bytes 6291456 | tf_op jit(solution)/shard_map/slice | solution.py:28
  137.1 3.2 broadcast_select_fusion.1
  140.4 3.9 %pad_maximum_fusion = f32[192,64,128]{0,2,1:T(8,128)} fusion(f32[192,64,64]{0,2,1:T(8,128)S(1)} %get-tuple-element.10, f32[192,64,64]{0,2,1:T(8,128)S(1)} %get-tuple-element.9), kind=kLoop, calls=%fused_computation.5 | loop fusion | flops 1572864 | bytes 12582912 | tf_op jit(solution)/shard_map/concatenate | solution.py:35
  144.3 8.7 %copy.19 = f32[192,8192]{1,0:T(8,128)} copy(f32[192,8192]{0,1:T(8,128)} %bitcast.42) | data formatting | bytes 12582912 | tf_op jit(solution)/shard_map/reshape | solution.py:37
  153.0 9.6 %fusion.6 = f32[24,64,12,128,1]{3,2,1,0,4:T(8,128)} fusion(s32[192]{0:T(256)S(1)} %fusion.25, s32[24,12]{1,0:T(8,128)S(1)} %multiply_add_fusion, f32[192,8192]{1,0:T(8,128)} %copy.19), kind=kOutput, calls=%fused_computation.10 | convolution fusion | flops 2717964288 | bytes 15730560 | tf_op jit(solution)/shard_map/dot_general | solution.py:42
  162.6 9.7 %copy.21 = f32[1536,12,128]{2,0,1:T(8,128)} copy(f32[1536,12,128]{0,2,1:T(8,128)} %bitcast.45) | data formatting | bytes 18874368 | tf_op jit(solution)/shard_map/dot_general | solution.py:47
  172.2 36.1 %fusion.7 = f32[24,64,12,128]{3,1,2,0:T(8,128)} fusion(f32[12,128,12,128]{3,1,0,2:T(8,128)} %bitcast.46, f32[24,64,12,128,1]{3,2,1,0,4:T(8,128)} %fusion.6), kind=kOutput, calls=%fused_computation.11 | convolution fusion | flops 21743271936 | bytes 28311552 | tf_op jit(solution)/shard_map/dot_general | solution.py:47
  208.4 8.2 %gather_fusion = f32[192,64,128]{2,1,0:T(8,128)} fusion(f32[24,64,12,128]{3,1,2,0:T(8,128)} %fusion.7, s32[192]{0:T(256)S(1)} %bitcast.44), kind=kCustom, calls=%fused_computation | custom fusion | bytes 12584448 | tf_op jit(solution)/shard_map/gather | solution.py:54
  216.5 8.5 %slice_select_fusion = f32[192,64,64]{2,1,0:T(8,128)} fusion(f32[192,64,128]{2,1,0:T(8,128)} %gather_fusion, pred[192]{0:T(512)(128)(4,1)S(1)} %get-tuple-element.5), kind=kLoop, calls=%fused_computation.9 | loop fusion | flops 786432 | bytes 9437376 | tf_op jit(solution)/shard_map/jit(_where)/select_n | solution.py:55
  225.0 7.1 %reshape.120 = f32[32,6,4096]{2,1,0:T(8,128)} reshape(f32[192,64,64]{2,1,0:T(8,128)} %slice_select_fusion) | data formatting | bytes 6291456 | tf_op jit(solution)/shard_map/reshape | solution.py:57
  232.1 101.8 %all_to_all.10 = f32[32,6,4096]{2,1,0:T(8,128)} all-to-all(f32[32,6,4096]{2,1,0:T(8,128)} %reshape.120), channel_id=1, replica_groups=mesh['pair'=32,'vir'=8] {'pair'}, dimensions={0} | all-to-all | bytes 6291456 | tf_op jit(solution)/shard_map/all_to_all | solution.py:58
  333.8 3.0 reshape.121
  336.8 2.5 fusion.20
  (12 shorter events, 0.4 us)
Async XLA Ops:
  6.5 156.0 %all-gather.2.cloned.1.call-start = ((), (), s32[]{:S(2)}) async-start(), calls=%async_computation.2 | async-start | bytes 10616832 | tf_op jit(solution)/shard_map/all_gather | solution.py:46
  15.5 111.3 %all-to-all-start = ((f32[32,6,4224]{2,1,0:T(8,128)}), f32[32,6,4224]{2,1,0:T(8,128)}, u32[]{:S(2)}, u32[]{:S(2)}) async-start(f32[32,6,4224]{2,1,0:T(8,128)} %reshape.115), calls=%async_computation | async-start | bytes 8650752 | tf_op jit(solution)/shard_map/all_to_all | solution.py:26
Sparse Core Ops, SparseCore 0:
  9.2 58.3 all-gather.1

commit v9 on v8

--- a/solution.py
+++ b/solution.py
@@ -29,12 +29,9 @@
     flat_keys = recv[:, TS * TS].astype(jnp.int32)
     row_block = flat_keys // NS
     col_block = flat_keys % NS
-    tiles = arrived.reshape(owner_count * capacity, TS, TS)
-    empty = jnp.zeros_like(tiles)
-    odd = (col_block % 2 == 1)[:, None, None]
-    halves = jnp.concatenate(
-        [jnp.where(odd, empty, tiles), jnp.where(odd, tiles, empty)], axis=2
-    ).reshape(owner_count * capacity, TS * 2 * TS)
+    tiles = arrived.reshape(owner_count * capacity, TS, 1, TS)
+    side = (jnp.arange(2, dtype=jnp.int32)[None, :] == (col_block % 2)[:, None])[:, None, :, None]
+    halves = jnp.where(side, tiles, 0.0).reshape(owner_count * capacity, TS * 2 * TS)
     places = jnp.arange(ROWSETS_DEV * NS // 2, dtype=jnp.int32)
     chooser = (places[:, None] == (row_block * (NS // 2) + col_block // 2)[None, :]).astype(
         jnp.float32

time: 347 us -> 336 us (0.968)
  local copies, waits for them, and re-layouts: 49.2 us -> 40.5 us
  other arithmetic: 18.7 us -> 15.1 us
    reshape x1 -> x0, local copies, waits for them, and re-layouts: 8.71 us -> none  [per_device(): halves = jnp.concatenate([jnp.where(odd, empty, tiles), jnp.where(odd, ti...]
    concatenate x1 -> x0, other arithmetic: 3.88 us -> none  [per_device(): jnp.concatenate([jnp.where(odd, empty, tiles), jnp.where(odd, tiles, empt...]
  transfers between devices with their start and end apart: 2 -> 2, of which waited for: 1 -> 1; matrix products, arithmetic and copies ran while one was open for 13% -> 10% of each run, Pallas kernels for 0% -> 0%
where the time goes in v9:
time: 336 us; the launch traced here: 335 us
  blocking collectives  102 us (30%)
  waiting for transfers between devices  101 us (30%)
  matrix products  52.2 us (16%)
  local copies, waits for them, and re-layouts  40.5 us (12%)
  other arithmetic  15.1 us (4%)
  between operations  13.5 us (4%)
  starting transfers between devices  11.4 us (3%)
    all_to_all x1, blocking collectives, per_device(): lax.all_to_all(answers, 'pair', split_axis=0, concat_axis=0, tiled=True)  102 us
    all_to_all x1, waiting for transfers between devices, per_device(): recv = lax.all_to_all(send, 'pair', split_axis=0, concat_axis=0, tiled=True)  99.8 us
    dot_general x1, matrix products, per_device(): lax.dot_general(blocked, right, (((2, 3), (0, 1)), ((), ())), precision=l...  36.1 us
    all_to_all x1, starting transfers between devices, per_device(): recv = lax.all_to_all(send, 'pair', split_axis=0, concat_axis=0, tiled=True)  11.4 us
    dot_general x1, matrix products, per_device(): jnp.dot(chooser, halves, precision=lax.Precision.HIGH, preferred_element_...  10.8 us
    dot_general x1, local copies, waits for them, and re-layouts, per_device(): lax.dot_general(blocked, right, (((2, 3), (0, 1)), ((), ())), precision=l...  9.66 us
    select_n x1, other arithmetic, per_device(): jnp.where((col_block % 2 == 0)[:, None, None], pairs[:, :, :TS], pairs[:,...  8.48 us
    gather x1, local copies, waits for them, and re-layouts, per_device(): product.reshape(ROWSETS_DEV, TS, NS // 2, 2 * TS)  8.15 us
  transfers between devices with their start and end apart: 2, of which 1 were waited for; matrix products, arithmetic and copies ran while one was open for 10% of the time, Pallas kernels for 0%

profile of v9, /device:TPU:16, one launch (start us, length us, event | category | flops | bytes accessed | tf_op | source)
XLA Modules:
  0.0 335.0 jit_solution(6973084315501004368)
XLA Ops:
  6.5 0.7 all-gather.2.cloned.1.call-update
  7.3 0.7 convert_element_type.24
  7.9 0.7 fusion.20
  8.7 0.1 reduce_window_sum.11
  8.8 0.8 select_reduce_fusion
  9.6 0.7 multiply_add_fusion.1
  10.4 2.8 fusion.9
  13.2 2.2 reshape.133
  15.5 11.4 %all-to-all-start = ((f32[32,6,4224]{2,1,0:T(8,128)}), f32[32,6,4224]{2,1,0:T(8,128)}, u32[]{:S(2)}, u32[]{:S(2)}) async-start(f32[32,6,4224]{2,1,0:T(8,128)} %reshape.133), calls=%async_computation | async-start | bytes 8650752 | tf_op jit(solution)/shard_map/all_to_all | solution.py:26
  26.9 99.8 %all-to-all-done = f32[32,6,4224]{2,1,0:T(8,128)} async-done(((f32[32,6,4224]{2,1,0:T(8,128)}), f32[32,6,4224]{2,1,0:T(8,128)}, u32[]{:S(2)}, u32[]{:S(2)}) %all-to-all-start) | async-done | bytes 3244064 | tf_op jit(solution)/shard_map/all_to_all | solution.py:26
  126.8 3.1 reshape.134
  129.8 2.0 slice.19
  131.9 0.1 copy.25
  131.9 5.1 %copy.13 = f32[192,4096]{0,1:T(8,128)} copy(f32[192,4096]{1,0:T(8,128)} %slice.19) | data formatting | bytes 6291456 | tf_op jit(solution)/shard_map/slice | solution.py:28
  137.2 3.5 %broadcast_select_fusion = f32[192,64,2,64]{0,3,2,1:T(8,128)S(1)} fusion(f32[192,64,64]{0,2,1:T(8,128)} %bitcast.36, pred[192,2]{0,1:T(4,128)(4,1)S(1)} %iota_compare_fusion.4), kind=kLoop, calls=%fused_computation.7 | loop fusion | flops 1572864 | bytes 9437568 | tf_op jit(solution)/shard_map/jit(_where)/select_n | solution.py:34
  140.7 10.8 %convolution_bitcast_fusion = f32[24,64,12,128,1]{3,2,1,0,4:T(8,128)} fusion(f32[64,128,192,1]{2,1,0,3:T(8,128)S(1)} %bitcast.35, s32[192]{0:T(256)S(1)} %fusion.22, s32[24,12]{1,0:T(8,128)S(1)} %multiply_add_fusion), kind=kOutput, calls=%fused_computation.6 | convolution fusion | flops 2717964288 | bytes 15730560 | tf_op jit(solution)/shard_map/dot_general | solution.py:39
  151.4 9.7 %copy.15 = f32[1536,12,128]{2,0,1:T(8,128)} copy(f32[1536,12,128]{0,2,1:T(8,128)} %bitcast.38) | data formatting | bytes 18874368 | tf_op jit(solution)/shard_map/dot_general | solution.py:44
  161.1 36.1 %fusion.4 = f32[24,64,12,128]{3,1,2,0:T(8,128)} fusion(f32[12,128,12,128]{3,1,0,2:T(8,128)} %bitcast.39, f32[24,64,12,128,1]{3,2,1,0,4:T(8,128)} %convolution_bitcast_fusion), kind=kOutput, calls=%fused_computation.8 | convolution fusion | flops 21743271936 | bytes 28311552 | tf_op jit(solution)/shard_map/dot_general | solution.py:44
  197.2 8.2 %gather_fusion = f32[192,64,128]{2,1,0:T(8,128)} fusion(f32[24,64,12,128]{3,1,2,0:T(8,128)} %fusion.4, s32[192]{0:T(256)S(1)} %bitcast.37), kind=kCustom, calls=%fused_computation | custom fusion | bytes 12584448 | tf_op jit(solution)/shard_map/gather | solution.py:51
  205.4 8.5 %slice_select_fusion = f32[192,64,64]{2,1,0:T(8,128)} fusion(f32[192,64,128]{2,1,0:T(8,128)} %gather_fusion, pred[192]{0:T(512)(128)(4,1)S(1)} %fusion.28), kind=kLoop, calls=%fused_computation.5 | loop fusion | flops 786432 | bytes 9437376 | tf_op jit(solution)/shard_map/jit(_where)/select_n | solution.py:52
  213.9 7.1 %reshape.136 = f32[32,6,4096]{2,1,0:T(8,128)} reshape(f32[192,64,64]{2,1,0:T(8,128)} %slice_select_fusion) | data formatting | bytes 6291456 | tf_op jit(solution)/shard_map/reshape | solution.py:54
  220.9 101.8 %all_to_all.10 = f32[32,6,4096]{2,1,0:T(8,128)} all-to-all(f32[32,6,4096]{2,1,0:T(8,128)} %reshape.136), channel_id=1, replica_groups=mesh['pair'=32,'vir'=8] {'pair'}, dimensions={0} | all-to-all | bytes 6291456 | tf_op jit(solution)/shard_map/all_to_all | solution.py:55
  322.7 3.0 reshape.137
  325.7 2.5 fusion.17
  (11 shorter events, 0.2 us)
Async XLA Ops:
  6.5 144.9 %all-gather.2.cloned.1.call-start = ((), (), s32[]{:S(2)}) async-start(), calls=%async_computation.2 | async-start | bytes 10616832 | tf_op jit(solution)/shard_map/all_gather | solution.py:43
  15.5 111.3 %all-to-all-start = ((f32[32,6,4224]{2,1,0:T(8,128)}), f32[32,6,4224]{2,1,0:T(8,128)}, u32[]{:S(2)}, u32[]{:S(2)}) async-start(f32[32,6,4224]{2,1,0:T(8,128)} %reshape.133), calls=%async_computation | async-start | bytes 8650752 | tf_op jit(solution)/shard_map/all_to_all | solution.py:26
Sparse Core Ops, SparseCore 0:
  9.2 58.3 all-gather.1

commit v10 on v9

--- a/solution.py
+++ b/solution.py
@@ -21,7 +21,7 @@
     key_lanes = jnp.broadcast_to(tile_key.astype(jnp.float32)[:, None], (tile_key.shape[0], 128))
     payload = jnp.concatenate([amplitudes, key_lanes], axis=1)
     send = jnp.dot(
-        packer, payload, precision=lax.Precision.HIGHEST, preferred_element_type=jnp.float32
+        packer, payload, precision=lax.Precision.HIGH, preferred_element_type=jnp.float32
     ).reshape(owner_count, capacity, TS * TS + 128)
     recv = lax.all_to_all(send, "pair", split_axis=0, concat_axis=0, tiled=True)
     recv = recv.reshape(owner_count * capacity, TS * TS + 128)
@@ -55,7 +55,7 @@
     returned = lax.all_to_all(answers, "pair", split_axis=0, concat_axis=0, tiled=True)
     returned = returned.reshape(owner_count * capacity, TS * TS)
     return jnp.dot(
-        packer.T, returned, precision=lax.Precision.HIGHEST, preferred_element_type=jnp.float32
+        packer.T, returned, precision=lax.Precision.HIGH, preferred_element_type=jnp.float32
     )
 
 

time: 336 us -> 335 us (level)
  no operation moved by 1% of the time
where the time goes in v10:
time: 335 us; the launch traced here: 334 us
  blocking collectives  102 us (30%)
  waiting for transfers between devices  101 us (30%)
  matrix products  51.2 us (15%)
  local copies, waits for them, and re-layouts  40.5 us (12%)
  other arithmetic  15.1 us (5%)
  between operations  13.5 us (4%)
  starting transfers between devices  11.4 us (3%)
    all_to_all x1, blocking collectives, per_device(): lax.all_to_all(answers, 'pair', split_axis=0, concat_axis=0, tiled=True)  102 us
    all_to_all x1, waiting for transfers between devices, per_device(): recv = lax.all_to_all(send, 'pair', split_axis=0, concat_axis=0, tiled=True)  99.8 us
    dot_general x1, matrix products, per_device(): lax.dot_general(blocked, right, (((2, 3), (0, 1)), ((), ())), precision=l...  36.1 us
    all_to_all x1, starting transfers between devices, per_device(): recv = lax.all_to_all(send, 'pair', split_axis=0, concat_axis=0, tiled=True)  11.4 us
    dot_general x1, matrix products, per_device(): jnp.dot(chooser, halves, precision=lax.Precision.HIGH, preferred_element_...  10.8 us
    dot_general x1, local copies, waits for them, and re-layouts, per_device(): lax.dot_general(blocked, right, (((2, 3), (0, 1)), ((), ())), precision=l...  9.66 us
    select_n x1, other arithmetic, per_device(): jnp.where((col_block % 2 == 0)[:, None, None], pairs[:, :, :TS], pairs[:,...  8.48 us
    gather x1, local copies, waits for them, and re-layouts, per_device(): product.reshape(ROWSETS_DEV, TS, NS // 2, 2 * TS)  8.15 us
  transfers between devices with their start and end apart: 2, of which 1 were waited for; matrix products, arithmetic and copies ran while one was open for 10% of the time, Pallas kernels for 0%

profile of v10, /device:TPU:16, one launch (start us, length us, event | category | flops | bytes accessed | tf_op | source)
XLA Modules:
  0.0 334.1 jit_solution(933564175462270552)
XLA Ops:
  6.5 0.7 all-gather.2.cloned.1.call-update
  7.3 0.7 convert_element_type.24
  7.9 0.7 fusion.20
  8.7 0.1 reduce_window_sum.11
  8.8 0.8 select_reduce_fusion
  9.6 0.7 multiply_add_fusion.1
  10.4 2.4 fusion.9
  12.8 2.2 reshape.133
  15.0 11.4 %all-to-all-start = ((f32[32,6,4224]{2,1,0:T(8,128)}), f32[32,6,4224]{2,1,0:T(8,128)}, u32[]{:S(2)}, u32[]{:S(2)}) async-start(f32[32,6,4224]{2,1,0:T(8,128)} %reshape.133), calls=%async_computation | async-start | bytes 8650752 | tf_op jit(solution)/shard_map/all_to_all | solution.py:26
  26.5 99.8 %all-to-all-done = f32[32,6,4224]{2,1,0:T(8,128)} async-done(((f32[32,6,4224]{2,1,0:T(8,128)}), f32[32,6,4224]{2,1,0:T(8,128)}, u32[]{:S(2)}, u32[]{:S(2)}) %all-to-all-start) | async-done | bytes 3244064 | tf_op jit(solution)/shard_map/all_to_all | solution.py:26
  126.3 3.1 reshape.134
  129.4 2.0 slice.19
  131.4 0.1 copy.25
  131.5 5.1 %copy.13 = f32[192,4096]{0,1:T(8,128)} copy(f32[192,4096]{1,0:T(8,128)} %slice.19) | data formatting | bytes 6291456 | tf_op jit(solution)/shard_map/slice | solution.py:28
  136.8 3.5 %broadcast_select_fusion = f32[192,64,2,64]{0,3,2,1:T(8,128)S(1)} fusion(f32[192,64,64]{0,2,1:T(8,128)} %bitcast.36, pred[192,2]{0,1:T(4,128)(4,1)S(1)} %iota_compare_fusion.4), kind=kLoop, calls=%fused_computation.7 | loop fusion | flops 1572864 | bytes 9437568 | tf_op jit(solution)/shard_map/jit(_where)/select_n | solution.py:34
  140.3 10.8 %convolution_bitcast_fusion = f32[24,64,12,128,1]{3,2,1,0,4:T(8,128)} fusion(f32[64,128,192,1]{2,1,0,3:T(8,128)S(1)} %bitcast.35, s32[192]{0:T(256)S(1)} %fusion.22, s32[24,12]{1,0:T(8,128)S(1)} %multiply_add_fusion), kind=kOutput, calls=%fused_computation.6 | convolution fusion | flops 2717964288 | bytes 15730560 | tf_op jit(solution)/shard_map/dot_general | solution.py:39
  151.0 9.7 %copy.15 = f32[1536,12,128]{2,0,1:T(8,128)} copy(f32[1536,12,128]{0,2,1:T(8,128)} %bitcast.38) | data formatting | bytes 18874368 | tf_op jit(solution)/shard_map/dot_general | solution.py:44
  160.7 36.1 %fusion.4 = f32[24,64,12,128]{3,1,2,0:T(8,128)} fusion(f32[12,128,12,128]{3,1,0,2:T(8,128)} %bitcast.39, f32[24,64,12,128,1]{3,2,1,0,4:T(8,128)} %convolution_bitcast_fusion), kind=kOutput, calls=%fused_computation.8 | convolution fusion | flops 21743271936 | bytes 28311552 | tf_op jit(solution)/shard_map/dot_general | solution.py:44
  196.8 8.2 %gather_fusion = f32[192,64,128]{2,1,0:T(8,128)} fusion(f32[24,64,12,128]{3,1,2,0:T(8,128)} %fusion.4, s32[192]{0:T(256)S(1)} %bitcast.37), kind=kCustom, calls=%fused_computation | custom fusion | bytes 12584448 | tf_op jit(solution)/shard_map/gather | solution.py:51
  205.0 8.5 %slice_select_fusion = f32[192,64,64]{2,1,0:T(8,128)} fusion(f32[192,64,128]{2,1,0:T(8,128)} %gather_fusion, pred[192]{0:T(512)(128)(4,1)S(1)} %fusion.28), kind=kLoop, calls=%fused_computation.5 | loop fusion | flops 786432 | bytes 9437376 | tf_op jit(solution)/shard_map/jit(_where)/select_n | solution.py:52
  213.4 7.1 %reshape.136 = f32[32,6,4096]{2,1,0:T(8,128)} reshape(f32[192,64,64]{2,1,0:T(8,128)} %slice_select_fusion) | data formatting | bytes 6291456 | tf_op jit(solution)/shard_map/reshape | solution.py:54
  220.5 101.8 %all_to_all.10 = f32[32,6,4096]{2,1,0:T(8,128)} all-to-all(f32[32,6,4096]{2,1,0:T(8,128)} %reshape.136), channel_id=1, replica_groups=mesh['pair'=32,'vir'=8] {'pair'}, dimensions={0} | all-to-all | bytes 6291456 | tf_op jit(solution)/shard_map/all_to_all | solution.py:55
  322.3 3.0 reshape.137
  325.3 1.9 fusion.17
  (11 shorter events, 0.2 us)
Async XLA Ops:
  6.5 144.5 %all-gather.2.cloned.1.call-start = ((), (), s32[]{:S(2)}) async-start(), calls=%async_computation.2 | async-start | bytes 10616832 | tf_op jit(solution)/shard_map/all_gather | solution.py:43
  15.0 111.3 %all-to-all-start = ((f32[32,6,4224]{2,1,0:T(8,128)}), f32[32,6,4224]{2,1,0:T(8,128)}, u32[]{:S(2)}, u32[]{:S(2)}) async-start(f32[32,6,4224]{2,1,0:T(8,128)} %reshape.133), calls=%async_computation | async-start | bytes 8650752 | tf_op jit(solution)/shard_map/all_to_all | solution.py:26
Sparse Core Ops, SparseCore 0:
  9.2 58.3 all-gather.1
